TPU v7x, 512 devices: a whole 4x4x16 slice. The times are simulated.
512 devices in a mesh: heads: 8 (over y, core), seq: 64 (over z, x).
Axes of the slice: x: 4, y: 4, z: 16, core: 2. Of those that a mesh axis runs over, the one named last changes fastest.
Arguments:
- query_proj: bfloat16 [8192, 4096], P('seq', 'heads'), may hold values from -6 to 6
- key_proj: bfloat16 [8192, 4096], P('seq', 'heads'), may hold values from -6 to 6
- value_proj: bfloat16 [8192, 4096], P('seq', 'heads'), may hold values from -6 to 6
- gate_proj: bfloat16 [8192, 4096], P('seq', 'heads'), may hold values from -6 to 6
- write_rate: float32 [32, 8192], P('heads', 'seq'), may hold values from 0 to 1
- log_decay: float32 [32, 8192], P('heads', 'seq'), may hold values from -1 to 0
- doc_start: int32 [8192], P('seq'), may hold values from 0 to 1, as said below
- norm_gain: float32 [128], replicated, may hold values from 0.5 to 1.5
- out_weight: bfloat16 [4096, 4096], P('heads', 'seq'), may hold values from -0.09375 to 0.09375
Outputs:
- layer_out: bfloat16 [8192, 4096], P('seq', 'heads')
Inputs may be any that keep to these rules, and one draw needn't show every extreme that they name: `doc_start`: exactly two entries are 1: one in the first half of the sequence (never token 0) and one in the second half.
All inputs are finite; a program needn't handle non-finite values.
Results may differ from a plain program's by a relative error of at most 0.017.
Values may be sent and summed in bfloat16 or wider, within the bound.
No kernel may reach another device: no remote copies, remote signals or barrier semaphores. Data moves between devices by JAX's collectives and lax.ppermute only.
A program may use at most 128 MiB of HBM per device.

v0:
```python
import jax
import jax.numpy as jnp
from jax import lax
from jax.sharding import PartitionSpec as P

STRETCH = 64


precise = lax.Precision.HIGHEST
epsilon = 1e-06


def prefix(part, axis, combine, identity):
    place = lax.axis_index(axis)
    gathered = jax.tree.map(lambda a: lax.all_gather(a, axis), part)
    state = jax.tree.map(lambda a, e: jnp.zeros_like(a) + jnp.asarray(e, a.dtype), part, identity)

    def one(lap, state):
        return combine(
            state, jax.tree.map(lambda a: lax.dynamic_index_in_dim(a, lap, 0, False), gathered)
        )

    return lax.fori_loop(0, place, one, state)


def unit_rows(block):
    return block / jnp.sqrt(jnp.sum(block * block, axis=-1, keepdims=True) + epsilon)


def triangular_inverse_below(system, right_side):
    return jax.scipy.linalg.solve_triangular(system, right_side, lower=True, unit_diagonal=True)


def matrix_product(left_side, right_side):
    return jnp.einsum("...de,...ef->...df", left_side, right_side, precision=precise)


def stretch_terms(queries, keys_normed, values_in, rates, decays, resets):
    length = queries.shape[-2]
    cumulated = jnp.cumsum(decays, axis=-1)
    seen = jnp.cumsum(resets, axis=-1)
    row_index = lax.broadcasted_iota(jnp.int32, (length, length), 0)
    col_index = lax.broadcasted_iota(jnp.int32, (length, length), 1)
    same_span = (seen[..., :, None] == seen[..., None, :]) & (row_index >= col_index)
    log_gap = jnp.where(same_span, cumulated[..., :, None] - cumulated[..., None, :], 0.0)
    pair_decay = jnp.where(same_span, jnp.exp(log_gap), 0.0)
    head_decay = jnp.exp(cumulated) * (seen == 0).astype(jnp.float32)
    tail_decay = jnp.exp(cumulated[..., -1:] - cumulated) * (seen[..., -1:] == seen).astype(
        jnp.float32
    )
    key_gram = jnp.einsum("...cd,...md->...cm", keys_normed, keys_normed, precision=precise)
    strict_part = jnp.where(row_index > col_index, rates[..., :, None] * pair_decay * key_gram, 0.0)
    system = strict_part + jnp.eye(length, dtype=jnp.float32)
    pseudo_values = triangular_inverse_below(system, rates[..., None] * values_in)
    key_weights = triangular_inverse_below(system, (rates * head_decay)[..., None] * keys_normed)
    scores = pair_decay * jnp.einsum("...cd,...md->...cm", queries, keys_normed, precision=precise)
    query_state = head_decay[..., None] * queries - jnp.einsum(
        "...cm,...md->...cd", scores, key_weights, precision=precise
    )
    local_out = jnp.einsum("...cm,...md->...cd", scores, pseudo_values, precision=precise)
    identity = jnp.eye(keys_normed.shape[-1], dtype=jnp.float32)
    transit = head_decay[..., -1][..., None, None] * identity - jnp.einsum(
        "...cd,...ce->...de", keys_normed, tail_decay[..., None] * key_weights, precision=precise
    )
    written = jnp.einsum(
        "...cd,...ce->...de", keys_normed, tail_decay[..., None] * pseudo_values, precision=precise
    )
    return (query_state, local_out, transit, written)


def gated_norm(core_out, gate_block, gain):
    scale = lax.rsqrt(jnp.mean(core_out * core_out, axis=-1, keepdims=True) + epsilon)
    gate_float = gate_block.astype(jnp.float32)
    return (core_out * scale * gain * jax.nn.silu(gate_float)).astype(jnp.bfloat16)


def compose_pairs(earlier, later_pair):
    return (
        matrix_product(later_pair[0], earlier[0]),
        matrix_product(later_pair[0], earlier[1]) + later_pair[1],
    )


def merge_states(reach, saved_state, empty_state, identity):
    leading_portion = prefix((reach, saved_state), "seq", compose_pairs, (identity, empty_state))
    return leading_portion[1]


def on_device(
    query_proj,
    key_proj,
    value_proj,
    gate_proj,
    write_rate,
    log_decay,
    doc_start,
    norm_gain,
    out_weight,
):
    tok_rows = query_proj.shape[0]
    head_count = write_rate.shape[0]
    key_width = query_proj.shape[1] // head_count
    value_width = value_proj.shape[1] // head_count
    blocks = tok_rows // STRETCH

    def stretch_major(array, width):
        return array.reshape(blocks, STRETCH, head_count, width).transpose(0, 2, 1, 3)

    queries = unit_rows(stretch_major(query_proj, key_width).astype(jnp.float32))
    keys_normed = unit_rows(stretch_major(key_proj, key_width).astype(jnp.float32))
    values_in = stretch_major(value_proj, value_width).astype(jnp.float32)
    rates = write_rate.reshape(head_count, blocks, STRETCH).transpose(1, 0, 2)
    decays = log_decay.reshape(head_count, blocks, STRETCH).transpose(1, 0, 2)
    resets = doc_start.reshape(blocks, 1, STRETCH)
    query_state, local_out, transit, written = stretch_terms(
        queries, keys_normed, values_in, rates, decays, resets
    )
    identity = jnp.broadcast_to(
        jnp.eye(key_width, dtype=jnp.float32), (head_count, key_width, key_width)
    )
    empty_state = jnp.zeros((head_count, key_width, value_width), jnp.float32)

    def compose_block(carried, transit_now, written_now):
        reach, saved_state = carried
        return (
            matrix_product(transit_now, reach),
            matrix_product(transit_now, saved_state) + written_now,
        )

    def gather_ends(carried, inputs):
        return (compose_block(carried, inputs[0], inputs[1]), None)

    ends, unused_out = lax.scan(gather_ends, (identity, empty_state), (transit, written))
    incoming = merge_states(ends[0], ends[1], empty_state, identity)

    def replay(state_now, inputs):
        query_now, local_now, transit_now, written_now = inputs
        block_out = jnp.einsum("hcd,hde->hce", query_now, state_now, precision=precise) + local_now
        return (matrix_product(transit_now, state_now) + written_now, block_out)

    unused_state, core_out = lax.scan(replay, incoming, (query_state, local_out, transit, written))
    core_tokens = core_out.transpose(0, 2, 1, 3).reshape(tok_rows, head_count, value_width)
    normed = gated_norm(
        core_tokens, gate_proj.reshape(tok_rows, head_count, value_width), norm_gain
    )
    normed = normed.reshape(tok_rows, head_count * value_width)
    partial_value = jnp.dot(
        normed,
        lax.all_gather(out_weight, "seq", axis=1, tiled=True),
        preferred_element_type=jnp.float32,
    )
    return lax.psum_scatter(
        partial_value.astype(jnp.bfloat16), "heads", scatter_dimension=1, tiled=True
    )


def solution(mesh):
    placed = (
        P("seq", "heads"),
        P("seq", "heads"),
        P("seq", "heads"),
        P("seq", "heads"),
        P("heads", "seq"),
        P("heads", "seq"),
        P("seq"),
        P(),
        P("heads", "seq"),
    )
    return jax.shard_map(
        on_device, mesh=mesh, in_specs=placed, out_specs=P("seq", "heads"), check_vma=False
    )
```

profile of v0, /device:TPU:6, one launch (start us, length us, event | category | flops | bytes accessed | tf_op | source)
XLA Modules:
  0.0 640.6 jit_solution(5498743281683938683)
XLA Ops:
  6.6 0.8 reshape.140
  7.4 0.5 reduce_window_sum.25
  8.0 1.0 reshape.143
  9.2 0.8 reshape.139
  10.0 0.5 reduce_window_sum.24
  10.6 0.8 reshape.141
  11.7 0.7 fusion.26
  12.4 39.3 %custom-call.5 = f32[2,4,1,64,64]{3,4,2,1,0:T(8,128)S(1)} custom-call(f32[2,4,1,64,64]{4,3,2,1,0:T(8,128)S(1)} %fusion.26), custom_call_target="InvertDiagBlocksLowerTriangular" | custom-call | tf_op jit(solution)/shard_map/jit(_solve_triangular)/vmap(vmap())/triangular_solve | solution.py:31
  51.7 1.0 reshape.144
  52.7 0.8 fusion.35
  53.5 0.7 fusion.33
  54.3 1.2 fusion.39
  55.5 1.2 convolution_subtract_fusion
  56.7 1.8 while.39
  56.7 0.4 convolution_add_fusion.9
  57.6 0.4 convolution_add_fusion.9
  58.5 0.7 copy-done.1
  59.3 0.7 all-gather.10.cloned.1.call-update
  60.0 0.7 all-gather.6.cloned.1.call-update
  61.0 0.7 convolution_multiply_fusion
  62.1 0.4 convolution_subtract_fusion.1
  62.5 192.2 %all-gather.8.cloned.1.call-done = f32[256,128,128]{2,1,0:T(8,128)} async-done(((f32[4,128,128]{2,1,0:T(8,128)}), f32[256,128,128]{2,1,0:T(8,128)}) %all-gather.8.cloned.1.call-update) | async-done | bytes 16777232 | tf_op jit(solution)/shard_map/all_gather | solution.py:15
  254.7 192.2 %all-gather.10.cloned.1.call-done = f32[256,128,128]{2,1,0:T(8,128)} async-done(((f32[4,128,128]{2,1,0:T(8,128)}), f32[256,128,128]{2,1,0:T(8,128)}) %all-gather.10.cloned.1.call-update) | async-done | bytes 16777232 | tf_op jit(solution)/shard_map/all_gather | solution.py:15
  446.9 4.5 while.37
  447.0 1.4 convolution_add_fusion.7
  448.5 1.4 convolution_add_fusion.7
  450.0 1.4 convolution_add_fusion.7
  451.4 1.6 while.38
  451.8 0.4 convolution_add_fusion.8
  453.5 139.0 %all-gather.6.cloned.1.call-done = bf16[512,4096]{0,1:T(8,128)(2,1)} async-done(((bf16[512,64]{0,1:T(8,128)(2,1)}), bf16[512,4096]{0,1:T(8,128)(2,1)}) %all-gather.6.cloned.1.call-update) | async-done | bytes 4194320 | tf_op jit(solution)/shard_map/all_gather | solution.py:149
  592.7 4.7 convolution_convert_fusion
  597.4 36.6 %reduce-scatter.2.cloned.1.call-done = bf16[128,512]{1,0:T(8,128)(2,1)} async-done(((bf16[128,4096]{1,0:T(8,128)(2,1)}), bf16[128,512]{1,0:T(8,128)(2,1)}) %reduce-scatter.2.cloned.1.call-update) | async-done | bytes 131088 | tf_op jit(solution)/shard_map/reduce_scatter | solution.py:152
  (57 shorter events, 4.6 us)
Async XLA Ops:
  6.5 54.5 %copy-start = (f32[128]{0:T(128)S(1)}, f32[128]{0:T(128)}, u32[]{:S(2)}) copy-start(f32[128]{0:T(128)} %param.24) | copy-start | bytes 1540
  6.5 54.2 %copy-start.3 = (bf16[128,512]{1,0:T(8,128)(2,1)S(1)}, bf16[128,512]{1,0:T(8,128)(2,1)}, u32[]{:S(2)}) copy-start(bf16[128,512]{1,0:T(8,128)(2,1)} %param.17) | copy-start | bytes 393220
  6.5 248.2 %all-gather.8.cloned.1.call-start = ((), (), s32[]{:S(2)}) async-start(), calls=%async_computation.3 | async-start | bytes 17039360 | tf_op jit(solution)/shard_map/all_gather | solution.py:15
  58.5 0.7 copy-start.1
  58.5 0.8 copy-start.2
  58.5 534.2 %copy-start.4 = (bf16[128,512]{1,0:T(8,128)(2,1)S(1)}, bf16[128,512]{1,0:T(8,128)(2,1)}, u32[]{:S(2)}) copy-start(bf16[128,512]{1,0:T(8,128)(2,1)} %param.20) | copy-start | bytes 393220
  59.2 387.7 %all-gather.10.cloned.1.call-start = ((), (), s32[]{:S(2)}) async-start(), calls=%async_computation.4 | async-start | bytes 17039360 | tf_op jit(solution)/shard_map/all_gather | solution.py:15
  59.9 532.6 %all-gather.6.cloned.1.call-start = ((), (), s32[]{:S(2)}) async-start(), calls=%async_computation.1 | async-start | bytes 4259840 | tf_op jit(solution)/shard_map/all_gather | solution.py:149
  60.7 573.3 %reduce-scatter.2.cloned.1.call-start = ((), (), s32[]{:S(2)}) async-start(), calls=%async_computation.2 | async-start | bytes 1179648 | tf_op jit(solution)/shard_map/reduce_scatter | solution.py:152
Sparse Core Ops, SparseCore 0:
  59.3 195.3 all-gather.7
  257.7 189.2 all-gather.9
  449.9 142.5 all-gather.5
  597.5 36.4 reduce-scatter.1
where the time goes:
time: 642 us; the launch traced here: 641 us
  waiting for transfers between devices  561 us (87%)
  other arithmetic  41.1 us (6%)
  matrix products  18 us (3%)
  between operations  13.4 us (2%)
    all_gather x2, waiting for transfers between devices, prefix(): gathered = jax.tree.map(lambda a: lax.all_gather(a, axis), part)  384 us
    all_gather x1, waiting for transfers between devices, on_device(): lax.all_gather(out_weight, 'seq', axis=1, tiled=True)  139 us
    another operation x3, other arithmetic, triangular_inverse_below(): jax.scipy.linalg.solve_triangular(system, right_side, lower=True, unit_di...  39.4 us
    reduce_scatter x1, waiting for transfers between devices, on_device(): lax.psum_scatter(partial_value.astype(jnp.bfloat16), 'heads', scatter_dim...  36.6 us
  transfers between devices with their start and end apart: 4, of which 4 were waited for; matrix products, arithmetic and copies ran while one was open for 1% of the time, Pallas kernels for 0%

commit v1 on v0

v1 whole, which is shorter than its diff:
```python
import jax
import jax.numpy as jnp
from jax import lax
from jax.sharding import Mesh
from jax.sharding import PartitionSpec as P

STRETCH = 64
SEQ_MINOR = 4


precise = lax.Precision.HIGHEST
epsilon = 1e-06


def unit_rows(block):
    return block / jnp.sqrt(jnp.sum(block * block, axis=-1, keepdims=True) + epsilon)


def triangular_inverse_below(system, right_side):
    return jax.scipy.linalg.solve_triangular(system, right_side, lower=True, unit_diagonal=True)


def matrix_product(left_side, right_side):
    return jnp.einsum("...de,...ef->...df", left_side, right_side, precision=precise)


def stretch_terms(queries, keys_normed, values_in, rates, decays, resets):
    length = queries.shape[-2]
    value_width = values_in.shape[-1]
    cumulated = jnp.cumsum(decays, axis=-1)
    seen = jnp.cumsum(resets, axis=-1)
    row_index = lax.broadcasted_iota(jnp.int32, (length, length), 0)
    col_index = lax.broadcasted_iota(jnp.int32, (length, length), 1)
    same_span = (seen[..., :, None] == seen[..., None, :]) & (row_index >= col_index)
    log_gap = jnp.where(same_span, cumulated[..., :, None] - cumulated[..., None, :], 0.0)
    pair_decay = jnp.where(same_span, jnp.exp(log_gap), 0.0)
    head_decay = jnp.exp(cumulated) * (seen == 0).astype(jnp.float32)
    tail_decay = jnp.exp(cumulated[..., -1:] - cumulated) * (seen[..., -1:] == seen).astype(
        jnp.float32
    )
    key_gram = jnp.einsum("...cd,...md->...cm", keys_normed, keys_normed, precision=precise)
    strict_part = jnp.where(row_index > col_index, rates[..., :, None] * pair_decay * key_gram, 0.0)
    system = strict_part + jnp.eye(length, dtype=jnp.float32)
    both_sides = jnp.concatenate(
        [rates[..., None] * values_in, (rates * head_decay)[..., None] * keys_normed], axis=-1
    )
    solved = triangular_inverse_below(system, both_sides)
    pseudo_values = solved[..., :value_width]
    key_weights = solved[..., value_width:]
    scores = pair_decay * jnp.einsum("...cd,...md->...cm", queries, keys_normed, precision=precise)
    query_state = head_decay[..., None] * queries - jnp.einsum(
        "...cm,...md->...cd", scores, key_weights, precision=precise
    )
    local_out = jnp.einsum("...cm,...md->...cd", scores, pseudo_values, precision=precise)
    identity = jnp.eye(keys_normed.shape[-1], dtype=jnp.float32)
    transit = head_decay[..., -1][..., None, None] * identity - jnp.einsum(
        "...cd,...ce->...de", keys_normed, tail_decay[..., None] * key_weights, precision=precise
    )
    written = jnp.einsum(
        "...cd,...ce->...de", keys_normed, tail_decay[..., None] * pseudo_values, precision=precise
    )
    return (query_state, local_out, transit, written)


def gated_norm(core_out, gate_block, gain):
    scale = lax.rsqrt(jnp.mean(core_out * core_out, axis=-1, keepdims=True) + epsilon)
    gate_float = gate_block.astype(jnp.float32)
    return (core_out * scale * gain * jax.nn.silu(gate_float)).astype(jnp.bfloat16)


def shift_down(array, step, fill):
    head = jnp.broadcast_to(fill, (step,) + array.shape[1:]).astype(array.dtype)
    return jnp.concatenate([head, array[:-step]], axis=0)


def on_device(
    query_proj,
    key_proj,
    value_proj,
    gate_proj,
    write_rate,
    log_decay,
    doc_start,
    norm_gain,
    out_weight,
    minor,
    major,
):
    head_count = write_rate.shape[0]
    key_width = query_proj.shape[1] // head_count
    value_width = value_proj.shape[1] // head_count

    def spread(array):
        return lax.all_to_all(array, "x", 1, 0, tiled=True)

    query_here = spread(query_proj)
    key_here = spread(key_proj)
    value_here = spread(value_proj)
    gate_here = spread(gate_proj)
    rates_here = lax.all_to_all(write_rate, "x", 0, 1, tiled=True)
    decays_here = lax.all_to_all(log_decay, "x", 0, 1, tiled=True)
    resets_here = lax.all_gather(doc_start, "x", tiled=True)

    tok_rows = query_here.shape[0]
    local_heads = head_count // minor
    blocks = tok_rows // STRETCH

    def stretch_major(array, width):
        return array.reshape(blocks, STRETCH, local_heads, width).transpose(0, 2, 1, 3)

    queries = unit_rows(stretch_major(query_here, key_width).astype(jnp.float32))
    keys_normed = unit_rows(stretch_major(key_here, key_width).astype(jnp.float32))
    values_in = stretch_major(value_here, value_width).astype(jnp.float32)
    rates = rates_here.reshape(local_heads, blocks, STRETCH).transpose(1, 0, 2)
    decays = decays_here.reshape(local_heads, blocks, STRETCH).transpose(1, 0, 2)
    resets = resets_here.reshape(blocks, 1, STRETCH)
    query_state, local_out, transit, written = stretch_terms(
        queries, keys_normed, values_in, rates, decays, resets
    )
    identity = jnp.eye(key_width, dtype=jnp.float32)

    reach, saved = transit, written
    step = 1
    while step < blocks:
        earlier_reach = shift_down(reach, step, identity)
        earlier_saved = shift_down(saved, step, 0.0)
        saved = matrix_product(reach, earlier_saved) + saved
        reach = matrix_product(reach, earlier_reach)
        step *= 2

    place = lax.axis_index("z")
    group_reach, group_saved = reach[-1], saved[-1]
    step = 1
    while step < major:
        pairs = [(i, i + step) for i in range(major - step)]
        if 2 * step < major:
            got = lax.ppermute(jnp.stack([group_reach, group_saved]), "z", pairs)
            got_reach, got_saved = got[0], got[1]
            new_saved = matrix_product(group_reach, got_saved) + group_saved
            group_reach = jnp.where(
                place >= step, matrix_product(group_reach, got_reach), group_reach
            )
        else:
            got_saved = lax.ppermute(group_saved, "z", pairs)
            new_saved = matrix_product(group_reach, got_saved) + group_saved
        group_saved = new_saved
        step *= 2
    incoming = lax.ppermute(group_saved, "z", [(i, i + 1) for i in range(major - 1)])

    entry_reach = shift_down(reach, 1, identity)
    entry_saved = shift_down(saved, 1, 0.0)
    entry_state = matrix_product(entry_reach, incoming[None]) + entry_saved
    core_out = (
        jnp.einsum("bhcd,bhde->bhce", query_state, entry_state, precision=precise) + local_out
    )
    core_tokens = core_out.transpose(0, 2, 1, 3).reshape(tok_rows, local_heads, value_width)
    normed = gated_norm(
        core_tokens, gate_here.reshape(tok_rows, local_heads, value_width), norm_gain
    )
    normed = normed.reshape(tok_rows, local_heads * value_width)
    normed = lax.all_to_all(normed, "x", 0, 1, tiled=True)
    partial_value = jnp.dot(
        normed,
        lax.all_gather(out_weight, ("z", "x"), axis=1, tiled=True),
        preferred_element_type=jnp.float32,
    )
    return lax.psum_scatter(
        partial_value.astype(jnp.bfloat16), "heads", scatter_dimension=1, tiled=True
    )


def solution(mesh):
    heads_size, seq_size = mesh.devices.shape
    minor = SEQ_MINOR
    major = seq_size // minor
    split_mesh = Mesh(mesh.devices.reshape(heads_size, major, minor), ("heads", "z", "x"))
    seq = ("z", "x")
    placed = (
        P(seq, "heads"),
        P(seq, "heads"),
        P(seq, "heads"),
        P(seq, "heads"),
        P("heads", seq),
        P("heads", seq),
        P(seq),
        P(),
        P("heads", seq),
    )

    def body(*arrays):
        return on_device(*arrays, minor=minor, major=major)

    return jax.shard_map(
        body, mesh=split_mesh, in_specs=placed, out_specs=P(seq, "heads"), check_vma=False
    )
```

time: 642 us -> 235 us (0.37)
  the two profiles are of different devices: /device:TPU:6 before, /device:TPU:4 now
where the time goes in v1:
time: 235 us
  starting transfers between devices  77 us (33%)
  waiting for transfers between devices  58.9 us (25%)
  other arithmetic  42.6 us (18%)
  blocking collectives  17.7 us (8%)
  matrix products  16.4 us (7%)
  between operations  13.9 us (6%)
  local copies, waits for them, and re-layouts  8.12 us (3%)
    reduce_scatter x1, waiting for transfers between devices, on_device(): lax.psum_scatter(partial_value.astype(jnp.bfloat16), 'heads', scatter_dim...  45 us
    another operation x2, other arithmetic, triangular_inverse_below(): jax.scipy.linalg.solve_triangular(system, right_side, lower=True, unit_di...  39.3 us
    ppermute x1, starting transfers between devices, on_device(): got_saved = lax.ppermute(group_saved, 'z', pairs)  21.5 us
    all_to_all x4, starting transfers between devices, spread(): return lax.all_to_all(array, 'x', 1, 0, tiled=True)  21.3 us
    ppermute x3, starting transfers between devices, on_device(): got = lax.ppermute(jnp.stack([group_reach, group_saved]), 'z', pairs)  17.9 us
    all_to_all x1, blocking collectives, on_device(): normed = lax.all_to_all(normed, 'x', 0, 1, tiled=True)  10 us
    all_to_all x1, starting transfers between devices, on_device(): decays_here = lax.all_to_all(log_decay, 'x', 0, 1, tiled=True)  9.17 us
    all_gather x1, blocking collectives, on_device(): resets_here = lax.all_gather(doc_start, 'x', tiled=True)  7.65 us
  transfers between devices with their start and end apart: 13, of which 7 were waited for; matrix products, arithmetic and copies ran while one was open for 27% of the time, Pallas kernels for 0%

profile of v1, /device:TPU:4, one launch (start us, length us, event | category | flops | bytes accessed | tf_op | source)
XLA Modules:
  0.0 234.6 jit_solution(6820988842869189103)
XLA Ops:
  6.5 9.2 %all-to-all-start = ((f32[4,1,128]{2,1,0:T(1,128)}), f32[4,1,128]{2,1,0:T(1,128)S(1)}, u32[]{:S(2)}, u32[]{:S(2)}) async-start(f32[4,1,128]{2,1,0:T(1,128)} %bitcast.231), calls=%async_computation | async-start | bytes 4096 | tf_op jit(solution)/shard_map/all_to_all | solution.py:101
  15.7 0.7 all-gather.3.cloned.1.call-update
  17.2 7.7 %all-gather = s32[4,1,128]{2,1,0:T(1,128)S(1)} all-gather(s32[1,1,128]{2,1,0:T(1,128)} %bitcast.233), channel_id=1, replica_groups=mesh['heads'=8,'z'=16,'x'=4] {'x'}, dimensions={0}, use_global_device_ids=true | all-gather | bytes 2560 | tf_op jit(solution)/shard_map/all_gather | solution.py:102
  26.4 1.6 copy_bitcast_fusion
  28.2 1.0 copy.59
  29.2 0.8 copy.60
  29.9 1.7 copy.69
  31.6 5.9 %all-to-all-start.3 = ((f32[4,1,128]{2,1,0:T(1,128)}), f32[4,1,128]{2,1,0:T(1,128)S(1)}, u32[]{:S(2)}, u32[]{:S(2)}) async-start(f32[4,1,128]{2,1,0:T(1,128)} %bitcast.232), calls=%async_computation.3 | async-start | bytes 4096 | tf_op jit(solution)/shard_map/all_to_all | solution.py:100
  39.1 1.3 all-to-all-done.3
  40.4 5.7 %all-to-all-start.2 = ((bf16[128,4,128]{2,0,1:T(8,128)(2,1)}), bf16[128,4,128]{2,0,1:T(8,128)(2,1)S(1)}, u32[]{:S(2)}, u32[]{:S(2)}) async-start(bf16[128,4,128]{2,0,1:T(8,128)(2,1)} %copy_bitcast_fusion.1), calls=%async_computation.2 | async-start | bytes 262144 | tf_op jit(solution)/shard_map/all_to_all | solution.py:94
  46.9 2.4 %all-to-all-done.2 = bf16[128,4,128]{2,0,1:T(8,128)(2,1)S(1)} async-done(((bf16[128,4,128]{2,0,1:T(8,128)(2,1)}), bf16[128,4,128]{2,0,1:T(8,128)(2,1)S(1)}, u32[]{:S(2)}, u32[]{:S(2)}) %all-to-all-start.2) | async-done | bytes 131104 | tf_op jit(solution)/shard_map/all_to_all | solution.py:94
  49.3 6.0 %all-to-all-start.4 = ((bf16[128,4,128]{2,0,1:T(8,128)(2,1)}), bf16[128,4,128]{2,0,1:T(8,128)(2,1)S(1)}, u32[]{:S(2)}, u32[]{:S(2)}) async-start(bf16[128,4,128]{2,0,1:T(8,128)(2,1)} %copy_bitcast_fusion), calls=%async_computation.4 | async-start | bytes 262144 | tf_op jit(solution)/shard_map/all_to_all | solution.py:94
  55.6 0.7 fusion.6
  56.3 39.3 %custom-call.4 = f32[8,1,64,64]{2,3,1,0:T(8,128)S(1)} custom-call(f32[8,1,64,64]{3,2,1,0:T(8,128)S(1)} %fusion.6), custom_call_target="InvertDiagBlocksLowerTriangular" | custom-call | tf_op jit(solution)/shard_map/jit(_solve_triangular)/vmap()/triangular_solve | solution.py:20
  95.6 4.8 %all-to-all-start.1 = ((bf16[128,4,128]{2,0,1:T(8,128)(2,1)}), bf16[128,4,128]{2,0,1:T(8,128)(2,1)S(1)}, u32[]{:S(2)}, u32[]{:S(2)}) async-start(bf16[128,4,128]{2,0,1:T(8,128)(2,1)} %copy.60), calls=%async_computation.1 | async-start | bytes 262144 | tf_op jit(solution)/shard_map/all_to_all | solution.py:94
  101.5 1.2 fusion.38
  102.7 1.2 convolution_subtract_fusion
  104.6 0.7 fusion.13
  108.0 1.3 collective-permute-start
  109.3 4.8 %all-to-all-start.5 = ((bf16[128,4,128]{0,2,1:T(8,128)(2,1)}), bf16[128,4,128]{0,2,1:T(8,128)(2,1)S(1)}, u32[]{:S(2)}, u32[]{:S(2)}) async-start(bf16[128,4,128]{0,2,1:T(8,128)(2,1)} %bitcast.67), calls=%async_computation.5 | async-start | bytes 262144 | tf_op jit(solution)/shard_map/all_to_all | solution.py:94
  114.4 0.7 convolution_multiply_fusion.1
  115.5 3.6 %collective-permute-start.1 = (f32[2,1,128,128]{3,2,1,0:T(8,128)S(1)}, f32[2,1,128,128]{3,2,1,0:T(8,128)S(1)}, u32[]{:S(2)}, u32[]{:S(2)}) collective-permute-start(f32[2,1,128,128]{3,2,1,0:T(8,128)S(1)} %pad_maximum_fusion.3), channel_id=1, source_target_pairs={{0,8},{4,12},{8,16},{12,20},{16,24},{20,28},{24,32},{28,36},{32,40... | collective-permute-start | bytes 393224 | tf_op jit(solution)/shard_map/ppermute | solution.py:137
  119.6 2.2 collective-permute-done.1
  122.3 12.9 %collective-permute-start.2 = (f32[2,1,128,128]{3,2,1,0:T(8,128)S(1)}, f32[2,1,128,128]{3,2,1,0:T(8,128)S(1)}, u32[]{:S(2)}, u32[]{:S(2)}) collective-permute-start(f32[2,1,128,128]{3,2,1,0:T(8,128)S(1)} %pad_maximum_fusion.4), channel_id=1, source_target_pairs={{0,16},{4,20},{8,24},{12,28},{16,32},{20,36},{24,40},{28,44},{32,4... | collective-permute-start | bytes 393224 | tf_op jit(solution)/shard_map/ppermute | solution.py:137
  135.3 3.5 %collective-permute-done.2 = f32[2,1,128,128]{3,2,1,0:T(8,128)S(1)} collective-permute-done((f32[2,1,128,128]{3,2,1,0:T(8,128)S(1)}, f32[2,1,128,128]{3,2,1,0:T(8,128)S(1)}, u32[]{:S(2)}, u32[]{:S(2)}) %collective-permute-start.2) | collective-permute-done | bytes 131104 | tf_op jit(solution)/shard_map/ppermute | solution.py:137
  139.0 21.5 %collective-permute-start.3 = (f32[1,128,128]{2,1,0:T(8,128)S(1)}, f32[1,128,128]{2,1,0:T(8,128)S(1)}, u32[]{:S(2)}, u32[]{:S(2)}) collective-permute-start(f32[1,128,128]{2,1,0:T(8,128)S(1)} %bitcast.226), channel_id=1, source_target_pairs={{0,32},{4,36},{8,40},{12,44},{16,48},{20,52},{24,56},{28,60},{1,33... | collective-permute-start | bytes 196616 | tf_op jit(solution)/shard_map/ppermute | solution.py:144
  160.7 1.9 collective-permute-done.3
  162.9 1.3 collective-permute-start.4
  164.2 1.8 collective-permute-done.4
  168.1 10.0 %all_to_all.94 = bf16[4,128,128]{1,2,0:T(8,128)(2,1)S(1)} all-to-all(bf16[4,128,128]{1,2,0:T(8,128)(2,1)S(1)} %fusion.45), channel_id=1, replica_groups=mesh['heads'=8,'z'=16,'x'=4] {'x'}, dimensions={0} | all-to-all | bytes 262144 | tf_op jit(solution)/shard_map/all_to_all | solution.py:161
  178.1 4.7 %convolution_convert_fusion = bf16[128,4096]{1,0:T(8,128)(2,1)} fusion(bf16[128,512]{0,1:T(8,128)(2,1)S(1)} %bitcast.223, bf16[512,4096]{0,1:T(8,128)(2,1)} %all-gather.3.cloned.1.call-done), kind=kOutput, calls=%fused_computation | convolution fusion | flops 537395200 | bytes 5373952 | tf_op jit(solution)/shard_map/dot_general | solution.py:162
  182.8 45.0 %reduce-scatter.2.cloned.1.call-done = bf16[128,512]{1,0:T(8,128)(2,1)} async-done(((bf16[128,4096]{1,0:T(8,128)(2,1)}), bf16[128,512]{1,0:T(8,128)(2,1)}) %reduce-scatter.2.cloned.1.call-update) | async-done | bytes 131088 | tf_op jit(solution)/shard_map/reduce_scatter | solution.py:167
  (82 shorter events, 13.8 us)
Async XLA Ops:
  6.5 10.0 %copy-start = (bf16[128,512]{1,0:T(8,128)(2,1)S(1)}, bf16[128,512]{1,0:T(8,128)(2,1)}, u32[]{:S(2)}) copy-start(bf16[128,512]{1,0:T(8,128)(2,1)} %param.10) | copy-start | bytes 393220
  6.5 25.1 %all-to-all-start = ((f32[4,1,128]{2,1,0:T(1,128)}), f32[4,1,128]{2,1,0:T(1,128)S(1)}, u32[]{:S(2)}, u32[]{:S(2)}) async-start(f32[4,1,128]{2,1,0:T(1,128)} %bitcast.231), calls=%async_computation | async-start | bytes 4096 | tf_op jit(solution)/shard_map/all_to_all | solution.py:101
  15.7 162.4 %all-gather.3.cloned.1.call-start = ((), (), s32[]{:S(2)}) async-start(), calls=%async_computation.8 | async-start | bytes 4259840 | tf_op jit(solution)/shard_map/all_gather | solution.py:164
  31.6 8.8 %all-to-all-start.3 = ((f32[4,1,128]{2,1,0:T(1,128)}), f32[4,1,128]{2,1,0:T(1,128)S(1)}, u32[]{:S(2)}, u32[]{:S(2)}) async-start(f32[4,1,128]{2,1,0:T(1,128)} %bitcast.232), calls=%async_computation.3 | async-start | bytes 4096 | tf_op jit(solution)/shard_map/all_to_all | solution.py:100
  40.4 8.9 %all-to-all-start.2 = ((bf16[128,4,128]{2,0,1:T(8,128)(2,1)}), bf16[128,4,128]{2,0,1:T(8,128)(2,1)S(1)}, u32[]{:S(2)}, u32[]{:S(2)}) async-start(bf16[128,4,128]{2,0,1:T(8,128)(2,1)} %copy_bitcast_fusion.1), calls=%async_computation.2 | async-start | bytes 262144 | tf_op jit(solution)/shard_map/all_to_all | solution.py:94
  49.3 46.3 %all-to-all-start.4 = ((bf16[128,4,128]{2,0,1:T(8,128)(2,1)}), bf16[128,4,128]{2,0,1:T(8,128)(2,1)S(1)}, u32[]{:S(2)}, u32[]{:S(2)}) async-start(bf16[128,4,128]{2,0,1:T(8,128)(2,1)} %copy_bitcast_fusion), calls=%async_computation.4 | async-start | bytes 262144 | tf_op jit(solution)/shard_map/all_to_all | solution.py:94
  95.6 13.7 %all-to-all-start.1 = ((bf16[128,4,128]{2,0,1:T(8,128)(2,1)}), bf16[128,4,128]{2,0,1:T(8,128)(2,1)S(1)}, u32[]{:S(2)}, u32[]{:S(2)}) async-start(bf16[128,4,128]{2,0,1:T(8,128)(2,1)} %copy.60), calls=%async_computation.1 | async-start | bytes 262144 | tf_op jit(solution)/shard_map/all_to_all | solution.py:94
  108.0 7.1 %collective-permute-start = (f32[2,1,128,128]{3,2,1,0:T(8,128)S(1)}, f32[2,1,128,128]{3,2,1,0:T(8,128)S(1)}, u32[]{:S(2)}, u32[]{:S(2)}) collective-permute-start(f32[2,1,128,128]{3,2,1,0:T(8,128)S(1)} %pad_maximum_fusion.2), channel_id=1, source_target_pairs={{0,4},{4,8},{8,12},{12,16},{16,20},{20,24},{24,28},{28,32},{32,36}... | collective-permute-start | bytes 393224 | tf_op jit(solution)/shard_map/ppermute | solution.py:137
  109.3 58.6 %all-to-all-start.5 = ((bf16[128,4,128]{0,2,1:T(8,128)(2,1)}), bf16[128,4,128]{0,2,1:T(8,128)(2,1)S(1)}, u32[]{:S(2)}, u32[]{:S(2)}) async-start(bf16[128,4,128]{0,2,1:T(8,128)(2,1)} %bitcast.67), calls=%async_computation.5 | async-start | bytes 262144 | tf_op jit(solution)/shard_map/all_to_all | solution.py:94
  114.1 113.7 %reduce-scatter.2.cloned.1.call-start = ((), (), s32[]{:S(2)}) async-start(), calls=%async_computation.9 | async-start | bytes 1179648 | tf_op jit(solution)/shard_map/reduce_scatter | solution.py:167
  115.5 6.3 %collective-permute-start.1 = (f32[2,1,128,128]{3,2,1,0:T(8,128)S(1)}, f32[2,1,128,128]{3,2,1,0:T(8,128)S(1)}, u32[]{:S(2)}, u32[]{:S(2)}) collective-permute-start(f32[2,1,128,128]{3,2,1,0:T(8,128)S(1)} %pad_maximum_fusion.3), channel_id=1, source_target_pairs={{0,8},{4,12},{8,16},{12,20},{16,24},{20,28},{24,32},{28,36},{32,40... | collective-permute-start | bytes 393224 | tf_op jit(solution)/shard_map/ppermute | solution.py:137
  119.2 48.8 %copy-start.1 = (f32[128]{0:T(128)S(1)}, f32[128]{0:T(128)}, u32[]{:S(2)}) copy-start(f32[128]{0:T(128)} %param.16) | copy-start | bytes 1540
  122.3 16.5 %collective-permute-start.2 = (f32[2,1,128,128]{3,2,1,0:T(8,128)S(1)}, f32[2,1,128,128]{3,2,1,0:T(8,128)S(1)}, u32[]{:S(2)}, u32[]{:S(2)}) collective-permute-start(f32[2,1,128,128]{3,2,1,0:T(8,128)S(1)} %pad_maximum_fusion.4), channel_id=1, source_target_pairs={{0,16},{4,20},{8,24},{12,28},{16,32},{20,36},{24,40},{28,44},{32,4... | collective-permute-start | bytes 393224 | tf_op jit(solution)/shard_map/ppermute | solution.py:137
  139.0 23.7 %collective-permute-start.3 = (f32[1,128,128]{2,1,0:T(8,128)S(1)}, f32[1,128,128]{2,1,0:T(8,128)S(1)}, u32[]{:S(2)}, u32[]{:S(2)}) collective-permute-start(f32[1,128,128]{2,1,0:T(8,128)S(1)} %bitcast.226), channel_id=1, source_target_pairs={{0,32},{4,36},{8,40},{12,44},{16,48},{20,52},{24,56},{28,60},{1,33... | collective-permute-start | bytes 196616 | tf_op jit(solution)/shard_map/ppermute | solution.py:144
  162.9 3.2 %collective-permute-start.4 = (f32[1,128,128]{2,1,0:T(8,128)S(1)}, f32[1,128,128]{2,1,0:T(8,128)S(1)}, u32[]{:S(2)}, u32[]{:S(2)}) collective-permute-start(f32[1,128,128]{2,1,0:T(8,128)S(1)} %fusion.7), channel_id=1, source_target_pairs={{0,4},{4,8},{8,12},{12,16},{16,20},{20,24},{24,28},{28,32},{32,36}... | collective-permute-start | bytes 196616 | tf_op jit(solution)/shard_map/ppermute | solution.py:148
Sparse Core Ops, SparseCore 0:
  19.4 151.3 all-gather.2
  182.9 44.7 reduce-scatter.1

commit v2 on v1

--- a/solution.py
+++ b/solution.py
@@ -6,6 +6,8 @@
 
 STRETCH = 64
 SEQ_MINOR = 4
+SPLIT_GATHER = True
+A2A_SCATTER = True
 
 
 precise = lax.Precision.HIGHEST
@@ -90,16 +92,14 @@
     key_width = query_proj.shape[1] // head_count
     value_width = value_proj.shape[1] // head_count
 
-    def spread(array):
-        return lax.all_to_all(array, "x", 1, 0, tiled=True)
-
-    query_here = spread(query_proj)
-    key_here = spread(key_proj)
-    value_here = spread(value_proj)
-    gate_here = spread(gate_proj)
-    rates_here = lax.all_to_all(write_rate, "x", 0, 1, tiled=True)
-    decays_here = lax.all_to_all(log_decay, "x", 0, 1, tiled=True)
-    resets_here = lax.all_gather(doc_start, "x", tiled=True)
+    projections = jnp.stack([query_proj, key_proj, value_proj, gate_proj])
+    projections = lax.all_to_all(projections, "x", 2, 1, tiled=True)
+    query_here, key_here, value_here, gate_here = (projections[i] for i in range(4))
+    resets_wide = jnp.broadcast_to(doc_start.astype(jnp.float32), write_rate.shape)
+    per_token = jnp.stack([write_rate, log_decay, resets_wide])
+    per_token = lax.all_to_all(per_token, "x", 1, 2, tiled=True)
+    rates_here, decays_here = per_token[0], per_token[1]
+    resets_here = per_token[2, 0].astype(jnp.int32)
 
     tok_rows = query_here.shape[0]
     local_heads = head_count // minor
@@ -159,14 +159,25 @@
     )
     normed = normed.reshape(tok_rows, local_heads * value_width)
     normed = lax.all_to_all(normed, "x", 0, 1, tiled=True)
-    partial_value = jnp.dot(
-        normed,
-        lax.all_gather(out_weight, ("z", "x"), axis=1, tiled=True),
-        preferred_element_type=jnp.float32,
-    )
-    return lax.psum_scatter(
-        partial_value.astype(jnp.bfloat16), "heads", scatter_dimension=1, tiled=True
-    )
+    if SPLIT_GATHER:
+        weight_rows = lax.all_gather(out_weight, "z", axis=1, tiled=True)
+        weight_rows = lax.all_gather(weight_rows, "x", axis=1, tiled=True)
+        row_count, col_count = weight_rows.shape
+        weight_rows = (
+            weight_rows.reshape(row_count, minor, major, col_count // (minor * major))
+            .transpose(0, 2, 1, 3)
+            .reshape(row_count, col_count)
+        )
+    else:
+        weight_rows = lax.all_gather(out_weight, ("z", "x"), axis=1, tiled=True)
+    partial_value = jnp.dot(normed, weight_rows, preferred_element_type=jnp.float32)
+    partial_value = partial_value.astype(jnp.bfloat16)
+    if A2A_SCATTER:
+        groups = lax.psum(1, "heads")
+        pieces = partial_value.reshape(partial_value.shape[0], groups, -1)
+        pieces = lax.all_to_all(pieces, "heads", 1, 1, tiled=True)
+        return jnp.sum(pieces.astype(jnp.float32), axis=1).astype(jnp.bfloat16)
+    return lax.psum_scatter(partial_value, "heads", scatter_dimension=1, tiled=True)
 
 
 def solution(mesh):

time: 235 us -> 192 us (0.82)
  the two profiles are of different devices: /device:TPU:4 before, /device:TPU:256 now
where the time goes in v2:
time: 192 us
  waiting for transfers between devices  67.6 us (35%)
  other arithmetic  45.2 us (24%)
  starting transfers between devices  22.1 us (12%)
  blocking collectives  20 us (10%)
  matrix products  15.3 us (8%)
  between operations  13.9 us (7%)
  local copies, waits for them, and re-layouts  7.69 us (4%)
    another operation x3, other arithmetic, triangular_inverse_below(): jax.scipy.linalg.solve_triangular(system, right_side, lower=True, unit_di...  39.3 us
    ppermute x3, waiting for transfers between devices, on_device(): got = lax.ppermute(jnp.stack([group_reach, group_saved]), 'z', pairs)  27.4 us
    all_to_all x1, blocking collectives, on_device(): pieces = lax.all_to_all(pieces, 'heads', 1, 1, tiled=True)  20 us
    ppermute x1, waiting for transfers between devices, on_device(): got_saved = lax.ppermute(group_saved, 'z', pairs)  13.4 us
    all_gather x1, waiting for transfers between devices, on_device(): weight_rows = lax.all_gather(out_weight, 'z', axis=1, tiled=True)  10.2 us
    ppermute x3, starting transfers between devices, on_device(): got = lax.ppermute(jnp.stack([group_reach, group_saved]), 'z', pairs)  7.5 us
    all_to_all x1, waiting for transfers between devices, on_device(): projections = lax.all_to_all(projections, 'x', 2, 1, tiled=True)  6.89 us
    dot_general x14, matrix products, matrix_product(): jnp.einsum('...de,...ef->...df', left_side, right_side, precision=precise)  5.74 us
  transfers between devices with their start and end apart: 10, of which 9 were waited for; matrix products, arithmetic and copies ran while one was open for 32% of the time, Pallas kernels for 0%

profile of v2, /device:TPU:256, one launch (start us, length us, event | category | flops | bytes accessed | tf_op | source)
XLA Modules:
  0.0 191.8 jit_solution(12633195912239895727)
XLA Ops:
  6.5 0.7 convert_element_type.123
  7.2 1.3 pad_maximum_fusion.6
  8.5 4.3 %all-to-all-start = ((f32[3,4,128]{2,0,1:T(4,128)}), f32[3,4,128]{2,0,1:T(4,128)S(1)}, u32[]{:S(2)}, u32[]{:S(2)}) async-start(f32[3,4,128]{2,0,1:T(4,128)} %pad_maximum_fusion.6), calls=%async_computation | async-start | bytes 16384 | tf_op jit(solution)/shard_map/all_to_all | solution.py:100
  12.8 0.7 all-gather.3.cloned.1.call-update
  13.7 1.2 pad_maximum_fusion.2
  14.8 1.1 copy.54
  15.9 2.2 %all-to-all-done = f32[3,4,128]{2,0,1:T(4,128)S(1)} async-done(((f32[3,4,128]{2,0,1:T(4,128)}), f32[3,4,128]{2,0,1:T(4,128)S(1)}, u32[]{:S(2)}, u32[]{:S(2)}) %all-to-all-start) | async-done | bytes 6176 | tf_op jit(solution)/shard_map/all_to_all | solution.py:100
  18.1 3.5 %all-to-all-start.1 = ((bf16[4,128,512]{1,0,2:T(4,128)(2,1)}), bf16[4,128,512]{1,0,2:T(4,128)(2,1)S(1)}, u32[]{:S(2)}, u32[]{:S(2)}) async-start(bf16[4,128,512]{1,0,2:T(4,128)(2,1)} %copy.54), calls=%async_computation.1 | async-start | bytes 1048576 | tf_op jit(solution)/shard_map/all_to_all | solution.py:96
  23.0 6.9 %all-to-all-done.1 = bf16[4,128,512]{1,0,2:T(4,128)(2,1)S(1)} async-done(((bf16[4,128,512]{1,0,2:T(4,128)(2,1)}), bf16[4,128,512]{1,0,2:T(4,128)(2,1)S(1)}, u32[]{:S(2)}, u32[]{:S(2)}) %all-to-all-start.1) | async-done | bytes 524320 | tf_op jit(solution)/shard_map/all_to_all | solution.py:96
  30.6 0.7 fusion.6
  31.3 39.3 %custom-call.4 = f32[8,1,64,64]{2,3,1,0:T(8,128)S(1)} custom-call(f32[8,1,64,64]{3,2,1,0:T(8,128)S(1)} %fusion.6), custom_call_target="InvertDiagBlocksLowerTriangular" | custom-call | tf_op jit(solution)/shard_map/jit(_solve_triangular)/vmap()/triangular_solve | solution.py:22
  71.5 1.2 fusion.38
  72.7 1.2 convolution_subtract_fusion
  75.2 10.2 %all-gather.3.cloned.1.call-done = bf16[512,1024]{0,1:T(8,128)(2,1)} async-done(((bf16[512,64]{0,1:T(8,128)(2,1)}), bf16[512,1024]{0,1:T(8,128)(2,1)}) %all-gather.3.cloned.1.call-update) | async-done | bytes 1048592 | tf_op jit(solution)/shard_map/all_gather | solution.py:163
  88.2 2.6 %collective-permute-start = (f32[2,1,128,128]{3,2,1,0:T(8,128)S(1)}, f32[2,1,128,128]{3,2,1,0:T(8,128)S(1)}, u32[]{:S(2)}, u32[]{:S(2)}) collective-permute-start(f32[2,1,128,128]{3,2,1,0:T(8,128)S(1)} %pad_maximum_fusion.3), channel_id=1, source_target_pairs={{0,4},{4,8},{8,12},{12,16},{16,20},{20,24},{24,28},{28,32},{32,36}... | collective-permute-start | bytes 393224 | tf_op jit(solution)/shard_map/ppermute | solution.py:137
  91.0 0.7 convolution_multiply_fusion.1
  91.7 4.5 %collective-permute-done = f32[2,1,128,128]{3,2,1,0:T(8,128)S(1)} collective-permute-done((f32[2,1,128,128]{3,2,1,0:T(8,128)S(1)}, f32[2,1,128,128]{3,2,1,0:T(8,128)S(1)}, u32[]{:S(2)}, u32[]{:S(2)}) %collective-permute-start) | collective-permute-done | bytes 131104 | tf_op jit(solution)/shard_map/ppermute | solution.py:137
  96.7 1.9 %collective-permute-start.1 = (f32[2,1,128,128]{3,2,1,0:T(8,128)S(1)}, f32[2,1,128,128]{3,2,1,0:T(8,128)S(1)}, u32[]{:S(2)}, u32[]{:S(2)}) collective-permute-start(f32[2,1,128,128]{3,2,1,0:T(8,128)S(1)} %pad_maximum_fusion.4), channel_id=1, source_target_pairs={{0,8},{4,12},{8,16},{12,20},{16,24},{20,28},{24,32},{28,36},{32,40... | collective-permute-start | bytes 393224 | tf_op jit(solution)/shard_map/ppermute | solution.py:137
  99.1 10.8 %collective-permute-done.1 = f32[2,1,128,128]{3,2,1,0:T(8,128)S(1)} collective-permute-done((f32[2,1,128,128]{3,2,1,0:T(8,128)S(1)}, f32[2,1,128,128]{3,2,1,0:T(8,128)S(1)}, u32[]{:S(2)}, u32[]{:S(2)}) %collective-permute-start.1) | collective-permute-done | bytes 131104 | tf_op jit(solution)/shard_map/ppermute | solution.py:137
  110.3 2.9 %collective-permute-start.2 = (f32[2,1,128,128]{3,2,1,0:T(8,128)S(1)}, f32[2,1,128,128]{3,2,1,0:T(8,128)S(1)}, u32[]{:S(2)}, u32[]{:S(2)}) collective-permute-start(f32[2,1,128,128]{3,2,1,0:T(8,128)S(1)} %pad_maximum_fusion.5), channel_id=1, source_target_pairs={{0,16},{4,20},{8,24},{12,28},{16,32},{20,36},{24,40},{28,44},{32,4... | collective-permute-start | bytes 393224 | tf_op jit(solution)/shard_map/ppermute | solution.py:137
  113.3 12.0 %collective-permute-done.2 = f32[2,1,128,128]{3,2,1,0:T(8,128)S(1)} collective-permute-done((f32[2,1,128,128]{3,2,1,0:T(8,128)S(1)}, f32[2,1,128,128]{3,2,1,0:T(8,128)S(1)}, u32[]{:S(2)}, u32[]{:S(2)}) %collective-permute-start.2) | collective-permute-done | bytes 131104 | tf_op jit(solution)/shard_map/ppermute | solution.py:137
  125.5 1.3 collective-permute-start.3
  127.1 13.4 %collective-permute-done.3 = f32[1,128,128]{2,1,0:T(8,128)S(1)} collective-permute-done((f32[1,128,128]{2,1,0:T(8,128)S(1)}, f32[1,128,128]{2,1,0:T(8,128)S(1)}, u32[]{:S(2)}, u32[]{:S(2)}) %collective-permute-start.3) | collective-permute-done | bytes 65568 | tf_op jit(solution)/shard_map/ppermute | solution.py:144
  140.7 1.9 %collective-permute-start.4 = (f32[1,128,128]{2,1,0:T(8,128)S(1)}, f32[1,128,128]{2,1,0:T(8,128)S(1)}, u32[]{:S(2)}, u32[]{:S(2)}) collective-permute-start(f32[1,128,128]{2,1,0:T(8,128)S(1)} %fusion.7), channel_id=1, source_target_pairs={{0,4},{4,8},{8,12},{12,16},{16,20},{20,24},{24,28},{28,32},{32,36}... | collective-permute-start | bytes 196616 | tf_op jit(solution)/shard_map/ppermute | solution.py:148
  142.6 5.4 %collective-permute-done.4 = f32[1,128,128]{2,1,0:T(8,128)S(1)} collective-permute-done((f32[1,128,128]{2,1,0:T(8,128)S(1)}, f32[1,128,128]{2,1,0:T(8,128)S(1)}, u32[]{:S(2)}, u32[]{:S(2)}) %collective-permute-start.4) | collective-permute-done | bytes 65568 | tf_op jit(solution)/shard_map/ppermute | solution.py:148
  150.0 0.8 fusion.45
  150.7 3.6 %all-to-all-start.2 = ((bf16[4,128,128]{1,2,0:T(8,128)(2,1)}), bf16[4,128,128]{1,2,0:T(8,128)(2,1)S(1)}, u32[]{:S(2)}, u32[]{:S(2)}) async-start(bf16[4,128,128]{1,2,0:T(8,128)(2,1)} %fusion.45), calls=%async_computation.2 | async-start | bytes 262144 | tf_op jit(solution)/shard_map/all_to_all | solution.py:161
  154.4 4.7 %copy.64 = bf16[512,16,4,64]{0,3,2,1:T(8,128)(2,1)} copy(bf16[512,16,4,64]{0,3,1,2:T(8,128)(2,1)} %bitcast.193) | data formatting | bytes 8388608 | tf_op jit(solution)/shard_map/transpose | solution.py:168
  159.0 1.3 all-to-all-done.2
  160.3 3.7 %convolution_convert_fusion = bf16[128,4096]{1,0:T(8,128)(2,1)S(1)} fusion(bf16[128,512]{0,1:T(8,128)(2,1)S(1)} %bitcast.210, bf16[512,4096]{0,1:T(8,128)(2,1)} %bitcast.192), kind=kOutput, calls=%fused_computation | convolution fusion | flops 537395200 | bytes 5373952 | tf_op jit(solution)/shard_map/dot_general | solution.py:173
  164.1 20.0 %all_to_all.45 = bf16[128,8,512]{2,0,1:T(8,128)(2,1)S(1)} all-to-all(bf16[128,8,512]{2,0,1:T(8,128)(2,1)S(1)} %bitcast.194), channel_id=1, replica_groups=mesh['heads'=8,'z'=16,'x'=4] {'heads'}, dimensions={1} | all-to-all | bytes 2097152 | tf_op jit(solution)/shard_map/all_to_all | solution.py:178
  184.1 0.8 reduce_sum.42
  (73 shorter events, 11.1 us)
Async XLA Ops:
  8.5 9.6 %all-to-all-start = ((f32[3,4,128]{2,0,1:T(4,128)}), f32[3,4,128]{2,0,1:T(4,128)S(1)}, u32[]{:S(2)}, u32[]{:S(2)}) async-start(f32[3,4,128]{2,0,1:T(4,128)} %pad_maximum_fusion.6), calls=%async_computation | async-start | bytes 16384 | tf_op jit(solution)/shard_map/all_to_all | solution.py:100
  12.8 72.6 %all-gather.3.cloned.1.call-start = ((), (), s32[]{:S(2)}) async-start(), calls=%async_computation.4 | async-start | bytes 1114112 | tf_op jit(solution)/shard_map/all_gather | solution.py:163
  18.1 11.8 %all-to-all-start.1 = ((bf16[4,128,512]{1,0,2:T(4,128)(2,1)}), bf16[4,128,512]{1,0,2:T(4,128)(2,1)S(1)}, u32[]{:S(2)}, u32[]{:S(2)}) async-start(bf16[4,128,512]{1,0,2:T(4,128)(2,1)} %copy.54), calls=%async_computation.1 | async-start | bytes 1048576 | tf_op jit(solution)/shard_map/all_to_all | solution.py:96
  21.6 132.8 %all-gather.5.cloned.1.call-start = ((), (), s32[]{:S(2)}) async-start(), calls=%async_computation.5 | async-start | bytes 5242880 | tf_op jit(solution)/shard_map/all_gather | solution.py:164
  88.2 8.1 %collective-permute-start = (f32[2,1,128,128]{3,2,1,0:T(8,128)S(1)}, f32[2,1,128,128]{3,2,1,0:T(8,128)S(1)}, u32[]{:S(2)}, u32[]{:S(2)}) collective-permute-start(f32[2,1,128,128]{3,2,1,0:T(8,128)S(1)} %pad_maximum_fusion.3), channel_id=1, source_target_pairs={{0,4},{4,8},{8,12},{12,16},{16,20},{20,24},{24,28},{28,32},{32,36}... | collective-permute-start | bytes 393224 | tf_op jit(solution)/shard_map/ppermute | solution.py:137
  96.7 13.2 %collective-permute-start.1 = (f32[2,1,128,128]{3,2,1,0:T(8,128)S(1)}, f32[2,1,128,128]{3,2,1,0:T(8,128)S(1)}, u32[]{:S(2)}, u32[]{:S(2)}) collective-permute-start(f32[2,1,128,128]{3,2,1,0:T(8,128)S(1)} %pad_maximum_fusion.4), channel_id=1, source_target_pairs={{0,8},{4,12},{8,16},{12,20},{16,24},{20,28},{24,32},{28,36},{32,40... | collective-permute-start | bytes 393224 | tf_op jit(solution)/shard_map/ppermute | solution.py:137
  98.6 51.3 %copy-start = (f32[128]{0:T(128)S(1)}, f32[128]{0:T(128)}, u32[]{:S(2)}) copy-start(f32[128]{0:T(128)} %param.16) | copy-start | bytes 1540
  110.3 15.0 %collective-permute-start.2 = (f32[2,1,128,128]{3,2,1,0:T(8,128)S(1)}, f32[2,1,128,128]{3,2,1,0:T(8,128)S(1)}, u32[]{:S(2)}, u32[]{:S(2)}) collective-permute-start(f32[2,1,128,128]{3,2,1,0:T(8,128)S(1)} %pad_maximum_fusion.5), channel_id=1, source_target_pairs={{0,16},{4,20},{8,24},{12,28},{16,32},{20,36},{24,40},{28,44},{32,4... | collective-permute-start | bytes 393224 | tf_op jit(solution)/shard_map/ppermute | solution.py:137
  125.5 14.9 %collective-permute-start.3 = (f32[1,128,128]{2,1,0:T(8,128)S(1)}, f32[1,128,128]{2,1,0:T(8,128)S(1)}, u32[]{:S(2)}, u32[]{:S(2)}) collective-permute-start(f32[1,128,128]{2,1,0:T(8,128)S(1)} %bitcast.213), channel_id=1, source_target_pairs={{0,32},{4,36},{8,40},{12,44},{16,48},{20,52},{24,56},{28,60},{1,33... | collective-permute-start | bytes 196616 | tf_op jit(solution)/shard_map/ppermute | solution.py:144
  140.7 7.4 %collective-permute-start.4 = (f32[1,128,128]{2,1,0:T(8,128)S(1)}, f32[1,128,128]{2,1,0:T(8,128)S(1)}, u32[]{:S(2)}, u32[]{:S(2)}) collective-permute-start(f32[1,128,128]{2,1,0:T(8,128)S(1)} %fusion.7), channel_id=1, source_target_pairs={{0,4},{4,8},{8,12},{12,16},{16,20},{20,24},{24,28},{28,32},{32,36}... | collective-permute-start | bytes 196616 | tf_op jit(solution)/shard_map/ppermute | solution.py:148
  150.7 9.6 %all-to-all-start.2 = ((bf16[4,128,128]{1,2,0:T(8,128)(2,1)}), bf16[4,128,128]{1,2,0:T(8,128)(2,1)S(1)}, u32[]{:S(2)}, u32[]{:S(2)}) async-start(bf16[4,128,128]{1,2,0:T(8,128)(2,1)} %fusion.45), calls=%async_computation.2 | async-start | bytes 262144 | tf_op jit(solution)/shard_map/all_to_all | solution.py:161
Sparse Core Ops, SparseCore 0:
  15.7 69.7 all-gather.2
  87.5 57.4 all-gather.4

commit v3 on v2

--- a/solution.py
+++ b/solution.py
@@ -6,8 +6,7 @@
 
 STRETCH = 64
 SEQ_MINOR = 4
-SPLIT_GATHER = True
-A2A_SCATTER = True
+INVERSE_BASE = 16
 
 
 precise = lax.Precision.HIGHEST
@@ -19,11 +18,52 @@
 
 
 def triangular_inverse_below(system, right_side):
-    return jax.scipy.linalg.solve_triangular(system, right_side, lower=True, unit_diagonal=True)
+    return matrix_product(unit_lower_inverse(system), right_side)
 
 
 def matrix_product(left_side, right_side):
     return jnp.einsum("...de,...ef->...df", left_side, right_side, precision=precise)
+
+
+def unit_lower_inverse(system):
+    size = system.shape[-1]
+    width = min(INVERSE_BASE, size)
+    count = size // width
+    identity = jnp.eye(width, dtype=system.dtype)
+    diagonal = jnp.stack(
+        [system[..., i * width : (i + 1) * width, i * width : (i + 1) * width] for i in range(count)],
+        axis=-3,
+    )
+    nilpotent = identity - diagonal
+    inverse = identity + nilpotent
+    power = 2
+    while power < width:
+        nilpotent = matrix_product(nilpotent, nilpotent)
+        inverse = matrix_product(inverse, identity + nilpotent)
+        power *= 2
+    while width < size:
+        pairs = count // 2
+        below = jnp.stack(
+            [
+                system[..., (2 * j + 1) * width : (2 * j + 2) * width, 2 * j * width : (2 * j + 1) * width]
+                for j in range(pairs)
+            ],
+            axis=-3,
+        )
+        upper_inverse = inverse[..., 0::2, :, :]
+        lower_inverse = inverse[..., 1::2, :, :]
+        corner = -matrix_product(matrix_product(lower_inverse, below), upper_inverse)
+        empty = jnp.zeros_like(upper_inverse)
+        inverse = jnp.concatenate(
+            [
+                jnp.concatenate([upper_inverse, empty], axis=-1),
+                jnp.concatenate([corner, lower_inverse], axis=-1),
+            ],
+            axis=-2,
+        )
+        width *= 2
+        count = pairs
+    return inverse[..., 0, :, :]
 
 
 def stretch_terms(queries, keys_normed, values_in, rates, decays, resets):
@@ -158,26 +198,17 @@
         core_tokens, gate_here.reshape(tok_rows, local_heads, value_width), norm_gain
     )
     normed = normed.reshape(tok_rows, local_heads * value_width)
-    normed = lax.all_to_all(normed, "x", 0, 1, tiled=True)
-    if SPLIT_GATHER:
-        weight_rows = lax.all_gather(out_weight, "z", axis=1, tiled=True)
-        weight_rows = lax.all_gather(weight_rows, "x", axis=1, tiled=True)
-        row_count, col_count = weight_rows.shape
-        weight_rows = (
-            weight_rows.reshape(row_count, minor, major, col_count // (minor * major))
-            .transpose(0, 2, 1, 3)
-            .reshape(row_count, col_count)
-        )
-    else:
-        weight_rows = lax.all_gather(out_weight, ("z", "x"), axis=1, tiled=True)
+    normed = lax.all_gather(normed, "x", axis=1, tiled=True)
+    groups = lax.psum(1, "heads")
+    weight_rows = lax.all_gather(out_weight, "z", axis=1, tiled=True)
     partial_value = jnp.dot(normed, weight_rows, preferred_element_type=jnp.float32)
     partial_value = partial_value.astype(jnp.bfloat16)
-    if A2A_SCATTER:
-        groups = lax.psum(1, "heads")
-        pieces = partial_value.reshape(partial_value.shape[0], groups, -1)
-        pieces = lax.all_to_all(pieces, "heads", 1, 1, tiled=True)
-        return jnp.sum(pieces.astype(jnp.float32), axis=1).astype(jnp.bfloat16)
-    return lax.psum_scatter(partial_value, "heads", scatter_dimension=1, tiled=True)
+    rows = tok_rows // minor
+    pieces = partial_value.reshape(minor, rows, groups, major // groups, -1)
+    pieces = lax.all_to_all(pieces, "heads", 2, 2, tiled=True)
+    summed = jnp.sum(pieces.astype(jnp.float32), axis=2).astype(jnp.bfloat16)
+    summed = lax.all_to_all(summed, "x", 0, 0, tiled=True)
+    return summed.transpose(1, 2, 0, 3).reshape(rows, -1)
 
 
 def solution(mesh):

time: 192 us -> 160 us (0.83)
  the two profiles are of different devices: /device:TPU:256 before, /device:TPU:385 now
where the time goes in v3:
time: 160 us; the launch traced here: 158 us
  waiting for transfers between devices  55.6 us (35%)
  blocking collectives  44.6 us (28%)
  matrix products  16.9 us (11%)
  starting transfers between devices  16.8 us (10%)
  between operations  14 us (9%)
  other arithmetic  5.22 us (3%)
  local copies, waits for them, and re-layouts  4.56 us (3%)
    ppermute x3, waiting for transfers between devices, on_device(): got = lax.ppermute(jnp.stack([group_reach, group_saved]), 'z', pairs)  31.5 us
    all_to_all x1, blocking collectives, on_device(): pieces = lax.all_to_all(pieces, 'heads', 2, 2, tiled=True)  24.9 us
    ppermute x1, waiting for transfers between devices, on_device(): got_saved = lax.ppermute(group_saved, 'z', pairs)  12.2 us
    all_gather x1, blocking collectives, on_device(): normed = lax.all_gather(normed, 'x', axis=1, tiled=True)  11.4 us
    dot_general x25, matrix products, matrix_product(): jnp.einsum('...de,...ef->...df', left_side, right_side, precision=precise)  9.66 us
    all_to_all x1, blocking collectives, on_device(): summed = lax.all_to_all(summed, 'x', 0, 0, tiled=True)  8.3 us
    ppermute x3, starting transfers between devices, on_device(): got = lax.ppermute(jnp.stack([group_reach, group_saved]), 'z', pairs)  6.1 us
    all_to_all x1, waiting for transfers between devices, on_device(): projections = lax.all_to_all(projections, 'x', 2, 1, tiled=True)  5.79 us
  transfers between devices with their start and end apart: 8, of which 7 were waited for; matrix products, arithmetic and copies ran while one was open for 13% of the time, Pallas kernels for 0%

profile of v3, /device:TPU:385, one launch (start us, length us, event | category | flops | bytes accessed | tf_op | source)
XLA Modules:
  0.0 157.6 jit_solution(6221467472681464886)
XLA Ops:
  6.5 0.7 convert_element_type.136
  7.2 1.3 pad_maximum_fusion.6
  8.5 4.0 %all-to-all-start = ((f32[3,4,128]{2,0,1:T(4,128)}), f32[3,4,128]{2,0,1:T(4,128)S(1)}, u32[]{:S(2)}, u32[]{:S(2)}) async-start(f32[3,4,128]{2,0,1:T(4,128)} %pad_maximum_fusion.6), calls=%async_computation | async-start | bytes 16384 | tf_op jit(solution)/shard_map/all_to_all | solution.py:140
  12.5 0.7 all-gather.2.cloned.1.call-update
  13.3 1.2 pad_maximum_fusion.2
  14.5 1.1 copy.50
  15.6 1.1 all-to-all-done
  16.7 3.5 %all-to-all-start.1 = ((bf16[4,128,512]{1,0,2:T(4,128)(2,1)}), bf16[4,128,512]{1,0,2:T(4,128)(2,1)S(1)}, u32[]{:S(2)}, u32[]{:S(2)}) async-start(bf16[4,128,512]{1,0,2:T(4,128)(2,1)} %copy.50), calls=%async_computation.1 | async-start | bytes 1048576 | tf_op jit(solution)/shard_map/all_to_all | solution.py:136
  21.5 5.8 %all-to-all-done.1 = bf16[4,128,512]{1,0,2:T(4,128)(2,1)S(1)} async-done(((bf16[4,128,512]{1,0,2:T(4,128)(2,1)}), bf16[4,128,512]{1,0,2:T(4,128)(2,1)S(1)}, u32[]{:S(2)}, u32[]{:S(2)}) %all-to-all-start.1) | async-done | bytes 524320 | tf_op jit(solution)/shard_map/all_to_all | solution.py:136
  28.1 0.7 fusion.4
  32.8 0.6 convolution_bitcast_fusion.1
  33.5 1.2 fusion.45
  34.7 1.2 convolution_subtract_fusion
  36.5 0.6 fusion.13
  37.9 0.7 fusion.20
  39.2 0.6 fusion.23
  39.9 2.8 %collective-permute-start = (f32[2,1,128,128]{3,2,1,0:T(8,128)S(1)}, f32[2,1,128,128]{3,2,1,0:T(8,128)S(1)}, u32[]{:S(2)}, u32[]{:S(2)}) collective-permute-start(f32[2,1,128,128]{3,2,1,0:T(8,128)S(1)} %pad_maximum_fusion.3), channel_id=1, source_target_pairs={{0,4},{4,8},{8,12},{12,16},{16,20},{20,24},{24,28},{28,32},{32,36}... | collective-permute-start | bytes 393224 | tf_op jit(solution)/shard_map/ppermute | solution.py:177
  42.8 0.7 convolution_multiply_fusion.1
  43.5 4.2 %collective-permute-done = f32[2,1,128,128]{3,2,1,0:T(8,128)S(1)} collective-permute-done((f32[2,1,128,128]{3,2,1,0:T(8,128)S(1)}, f32[2,1,128,128]{3,2,1,0:T(8,128)S(1)}, u32[]{:S(2)}, u32[]{:S(2)}) %collective-permute-start) | collective-permute-done | bytes 131104 | tf_op jit(solution)/shard_map/ppermute | solution.py:177
  48.1 2.0 %collective-permute-start.1 = (f32[2,1,128,128]{3,2,1,0:T(8,128)S(1)}, f32[2,1,128,128]{3,2,1,0:T(8,128)S(1)}, u32[]{:S(2)}, u32[]{:S(2)}) collective-permute-start(f32[2,1,128,128]{3,2,1,0:T(8,128)S(1)} %pad_maximum_fusion.4), channel_id=1, source_target_pairs={{0,8},{4,12},{8,16},{12,20},{16,24},{20,28},{24,32},{28,36},{32,40... | collective-permute-start | bytes 393224 | tf_op jit(solution)/shard_map/ppermute | solution.py:177
  50.6 6.9 %collective-permute-done.1 = f32[2,1,128,128]{3,2,1,0:T(8,128)S(1)} collective-permute-done((f32[2,1,128,128]{3,2,1,0:T(8,128)S(1)}, f32[2,1,128,128]{3,2,1,0:T(8,128)S(1)}, u32[]{:S(2)}, u32[]{:S(2)}) %collective-permute-start.1) | collective-permute-done | bytes 131104 | tf_op jit(solution)/shard_map/ppermute | solution.py:177
  57.9 1.3 collective-permute-start.2
  59.3 20.4 %collective-permute-done.2 = f32[2,1,128,128]{3,2,1,0:T(8,128)S(1)} collective-permute-done((f32[2,1,128,128]{3,2,1,0:T(8,128)S(1)}, f32[2,1,128,128]{3,2,1,0:T(8,128)S(1)}, u32[]{:S(2)}, u32[]{:S(2)}) %collective-permute-start.2) | collective-permute-done | bytes 131104 | tf_op jit(solution)/shard_map/ppermute | solution.py:177
  79.9 1.3 collective-permute-start.3
  81.4 12.2 %collective-permute-done.3 = f32[1,128,128]{2,1,0:T(8,128)S(1)} collective-permute-done((f32[1,128,128]{2,1,0:T(8,128)S(1)}, f32[1,128,128]{2,1,0:T(8,128)S(1)}, u32[]{:S(2)}, u32[]{:S(2)}) %collective-permute-start.3) | collective-permute-done | bytes 65568 | tf_op jit(solution)/shard_map/ppermute | solution.py:184
  93.8 1.9 %collective-permute-start.4 = (f32[1,128,128]{2,1,0:T(8,128)S(1)}, f32[1,128,128]{2,1,0:T(8,128)S(1)}, u32[]{:S(2)}, u32[]{:S(2)}) collective-permute-start(f32[1,128,128]{2,1,0:T(8,128)S(1)} %fusion.7), channel_id=1, source_target_pairs={{0,4},{4,8},{8,12},{12,16},{16,20},{20,24},{24,28},{28,32},{32,36}... | collective-permute-start | bytes 196616 | tf_op jit(solution)/shard_map/ppermute | solution.py:188
  95.8 4.3 %collective-permute-done.4 = f32[1,128,128]{2,1,0:T(8,128)S(1)} collective-permute-done((f32[1,128,128]{2,1,0:T(8,128)S(1)}, f32[1,128,128]{2,1,0:T(8,128)S(1)}, u32[]{:S(2)}, u32[]{:S(2)}) %collective-permute-start.4) | collective-permute-done | bytes 65568 | tf_op jit(solution)/shard_map/ppermute | solution.py:188
  102.0 11.4 %all_gather.6 = bf16[512,512]{1,0:T(8,128)(2,1)S(1)} all-gather(bf16[512,128]{1,0:T(8,128)(2,1)S(1)} %fusion.59), channel_id=1, replica_groups=mesh['heads'=8,'z'=16,'x'=4] {'x'}, dimensions={1}, use_global_device_ids=true | all-gather | bytes 655360 | tf_op jit(solution)/shard_map/all_gather | solution.py:201
  113.4 2.0 %convolution_convert_fusion = bf16[512,1024]{1,0:T(8,128)(2,1)S(1)} fusion(bf16[512,512]{1,0:T(8,128)(2,1)S(1)} %all_gather.6, bf16[512,1024]{0,1:T(8,128)(2,1)} %all-gather.2.cloned.1.call-done), kind=kOutput, calls=%fused_computation | convolution fusion | flops 537395200 | bytes 2621440 | tf_op jit(solution)/shard_map/dot_general | solution.py:204
  116.2 24.9 %all_to_all.34 = bf16[4,128,8,2,64]{1,0,4,3,2:T(4,128)(2,1)S(1)} all-to-all(bf16[4,128,8,2,64]{1,0,4,3,2:T(4,128)(2,1)S(1)} %reshape.672), channel_id=1, replica_groups=mesh['heads'=8,'z'=16,'x'=4] {'heads'}, dimensions={2} | all-to-all | bytes 2097152 | tf_op jit(solution)/shard_map/all_to_all | solution.py:208
  141.7 8.3 %all_to_all.35 = bf16[4,128,2,64]{1,3,2,0:T(8,128)(2,1)S(1)} all-to-all(bf16[4,128,2,64]{1,3,2,0:T(8,128)(2,1)S(1)} %copy.66), channel_id=1, replica_groups=mesh['heads'=8,'z'=16,'x'=4] {'x'}, dimensions={0} | all-to-all | bytes 262144 | tf_op jit(solution)/shard_map/all_to_all | solution.py:210
  150.0 0.8 copy.68
  (82 shorter events, 13.4 us)
Async XLA Ops:
  8.5 8.2 %all-to-all-start = ((f32[3,4,128]{2,0,1:T(4,128)}), f32[3,4,128]{2,0,1:T(4,128)S(1)}, u32[]{:S(2)}, u32[]{:S(2)}) async-start(f32[3,4,128]{2,0,1:T(4,128)} %pad_maximum_fusion.6), calls=%async_computation | async-start | bytes 16384 | tf_op jit(solution)/shard_map/all_to_all | solution.py:140
  12.5 100.8 %all-gather.2.cloned.1.call-start = ((), (), s32[]{:S(2)}) async-start(), calls=%async_computation.4 | async-start | bytes 1114112 | tf_op jit(solution)/shard_map/all_gather | solution.py:203
  16.7 10.6 %all-to-all-start.1 = ((bf16[4,128,512]{1,0,2:T(4,128)(2,1)}), bf16[4,128,512]{1,0,2:T(4,128)(2,1)S(1)}, u32[]{:S(2)}, u32[]{:S(2)}) async-start(bf16[4,128,512]{1,0,2:T(4,128)(2,1)} %copy.50), calls=%async_computation.1 | async-start | bytes 1048576 | tf_op jit(solution)/shard_map/all_to_all | solution.py:136
  39.9 7.8 %collective-permute-start = (f32[2,1,128,128]{3,2,1,0:T(8,128)S(1)}, f32[2,1,128,128]{3,2,1,0:T(8,128)S(1)}, u32[]{:S(2)}, u32[]{:S(2)}) collective-permute-start(f32[2,1,128,128]{3,2,1,0:T(8,128)S(1)} %pad_maximum_fusion.3), channel_id=1, source_target_pairs={{0,4},{4,8},{8,12},{12,16},{16,20},{20,24},{24,28},{28,32},{32,36}... | collective-permute-start | bytes 393224 | tf_op jit(solution)/shard_map/ppermute | solution.py:177
  48.1 9.3 %collective-permute-start.1 = (f32[2,1,128,128]{3,2,1,0:T(8,128)S(1)}, f32[2,1,128,128]{3,2,1,0:T(8,128)S(1)}, u32[]{:S(2)}, u32[]{:S(2)}) collective-permute-start(f32[2,1,128,128]{3,2,1,0:T(8,128)S(1)} %pad_maximum_fusion.4), channel_id=1, source_target_pairs={{0,8},{4,12},{8,16},{12,20},{16,24},{20,28},{24,32},{28,36},{32,40... | collective-permute-start | bytes 393224 | tf_op jit(solution)/shard_map/ppermute | solution.py:177
  57.9 21.7 %collective-permute-start.2 = (f32[2,1,128,128]{3,2,1,0:T(8,128)S(1)}, f32[2,1,128,128]{3,2,1,0:T(8,128)S(1)}, u32[]{:S(2)}, u32[]{:S(2)}) collective-permute-start(f32[2,1,128,128]{3,2,1,0:T(8,128)S(1)} %pad_maximum_fusion.5), channel_id=1, source_target_pairs={{0,16},{4,20},{8,24},{12,28},{16,32},{20,36},{24,40},{28,44},{32,4... | collective-permute-start | bytes 393224 | tf_op jit(solution)/shard_map/ppermute | solution.py:177
  79.9 13.7 %collective-permute-start.3 = (f32[1,128,128]{2,1,0:T(8,128)S(1)}, f32[1,128,128]{2,1,0:T(8,128)S(1)}, u32[]{:S(2)}, u32[]{:S(2)}) collective-permute-start(f32[1,128,128]{2,1,0:T(8,128)S(1)} %bitcast.242), channel_id=1, source_target_pairs={{0,32},{4,36},{8,40},{12,44},{16,48},{20,52},{24,56},{28,60},{1,33... | collective-permute-start | bytes 196616 | tf_op jit(solution)/shard_map/ppermute | solution.py:184
  93.8 6.2 %collective-permute-start.4 = (f32[1,128,128]{2,1,0:T(8,128)S(1)}, f32[1,128,128]{2,1,0:T(8,128)S(1)}, u32[]{:S(2)}, u32[]{:S(2)}) collective-permute-start(f32[1,128,128]{2,1,0:T(8,128)S(1)} %fusion.7), channel_id=1, source_target_pairs={{0,4},{4,8},{8,12},{12,16},{16,20},{20,24},{24,28},{28,32},{32,36}... | collective-permute-start | bytes 196616 | tf_op jit(solution)/shard_map/ppermute | solution.py:188
  100.6 1.2 copy-start
Sparse Core Ops, SparseCore 0:
  15.4 62.5 all-gather.1

commit v4 on v3

--- a/solution.py
+++ b/solution.py
@@ -7,6 +7,8 @@
 STRETCH = 64
 SEQ_MINOR = 4
 INVERSE_BASE = 16
+GATHER_AS_A2A = True
+JOINT_A2A = True
 
 
 precise = lax.Precision.HIGHEST
@@ -198,16 +200,27 @@
         core_tokens, gate_here.reshape(tok_rows, local_heads, value_width), norm_gain
     )
     normed = normed.reshape(tok_rows, local_heads * value_width)
-    normed = lax.all_gather(normed, "x", axis=1, tiled=True)
+    if GATHER_AS_A2A:
+        copies = jnp.broadcast_to(normed[None], (minor,) + normed.shape)
+        normed = lax.all_to_all(copies, "x", 0, 0, tiled=True)
+        normed = normed.transpose(1, 0, 2).reshape(tok_rows, -1)
+    else:
+        normed = lax.all_gather(normed, "x", axis=1, tiled=True)
     groups = lax.psum(1, "heads")
     weight_rows = lax.all_gather(out_weight, "z", axis=1, tiled=True)
     partial_value = jnp.dot(normed, weight_rows, preferred_element_type=jnp.float32)
     partial_value = partial_value.astype(jnp.bfloat16)
     rows = tok_rows // minor
     pieces = partial_value.reshape(minor, rows, groups, major // groups, -1)
-    pieces = lax.all_to_all(pieces, "heads", 2, 2, tiled=True)
-    summed = jnp.sum(pieces.astype(jnp.float32), axis=2).astype(jnp.bfloat16)
-    summed = lax.all_to_all(summed, "x", 0, 0, tiled=True)
+    if JOINT_A2A:
+        pieces = pieces.transpose(0, 2, 1, 3, 4).reshape(minor * groups, rows, major // groups, -1)
+        pieces = lax.all_to_all(pieces, ("x", "heads"), 0, 0, tiled=True)
+        pieces = pieces.reshape(minor, groups, rows, major // groups, -1)
+        summed = jnp.sum(pieces.astype(jnp.float32), axis=1).astype(jnp.bfloat16)
+    else:
+        pieces = lax.all_to_all(pieces, "heads", 2, 2, tiled=True)
+        summed = jnp.sum(pieces.astype(jnp.float32), axis=2).astype(jnp.bfloat16)
+        summed = lax.all_to_all(summed, "x", 0, 0, tiled=True)
     return summed.transpose(1, 2, 0, 3).reshape(rows, -1)
 
 

time: 160 us -> 151 us (0.944); the launches traced: 158 us -> 150 us
  blocking collectives: 44.6 us -> 37.5 us
    all_gather x1 -> x0, blocking collectives: 11.4 us -> none  [on_device(): normed = lax.all_gather(normed, 'x', axis=1, tiled=True)]
    all_to_all x2, blocking collectives: 33.2 us -> 37.5 us  [the longest x1 28.2 us: on_device(): pieces = lax.all_to_all(pieces, ('x', 'heads'), 0, 0, tiled=True)]
  transfers between devices with their start and end apart: 8 -> 8, of which waited for: 7 -> 7; matrix products, arithmetic and copies ran while one was open for 13% -> 14% of each run, Pallas kernels for 0% -> 0%
where the time goes in v4:
time: 151 us; the launch traced here: 150 us
  waiting for transfers between devices  55.3 us (37%)
  blocking collectives  37.5 us (25%)
  starting transfers between devices  16.9 us (11%)
  matrix products  16.9 us (11%)
  between operations  14 us (9%)
  local copies, waits for them, and re-layouts  4.95 us (3%)
  other arithmetic  4.83 us (3%)
    ppermute x3, waiting for transfers between devices, on_device(): got = lax.ppermute(jnp.stack([group_reach, group_saved]), 'z', pairs)  31.2 us
    all_to_all x1, blocking collectives, on_device(): pieces = lax.all_to_all(pieces, ('x', 'heads'), 0, 0, tiled=True)  28.2 us
    ppermute x1, waiting for transfers between devices, on_device(): got_saved = lax.ppermute(group_saved, 'z', pairs)  12.2 us
    dot_general x25, matrix products, matrix_product(): jnp.einsum('...de,...ef->...df', left_side, right_side, precision=precise)  9.66 us
    all_to_all x1, blocking collectives, on_device(): normed = lax.all_to_all(copies, 'x', 0, 0, tiled=True)  9.33 us
    ppermute x3, starting transfers between devices, on_device(): got = lax.ppermute(jnp.stack([group_reach, group_saved]), 'z', pairs)  6.17 us
    all_to_all x1, waiting for transfers between devices, on_device(): projections = lax.all_to_all(projections, 'x', 2, 1, tiled=True)  5.79 us
    ppermute x1, waiting for transfers between devices, on_device(): lax.ppermute(group_saved, 'z', [(i, i + 1) for i in range(major - 1)])  4.25 us
  transfers between devices with their start and end apart: 8, of which 7 were waited for; matrix products, arithmetic and copies ran while one was open for 14% of the time, Pallas kernels for 0%

profile of v4, /device:TPU:385, one launch (start us, length us, event | category | flops | bytes accessed | tf_op | source)
XLA Modules:
  0.0 150.3 jit_solution(2121956700186750148)
XLA Ops:
  6.5 0.7 convert_element_type.142
  7.2 1.3 pad_maximum_fusion.6
  8.5 4.0 %all-to-all-start = ((f32[3,4,128]{2,0,1:T(4,128)}), f32[3,4,128]{2,0,1:T(4,128)S(1)}, u32[]{:S(2)}, u32[]{:S(2)}) async-start(f32[3,4,128]{2,0,1:T(4,128)} %pad_maximum_fusion.6), calls=%async_computation | async-start | bytes 16384 | tf_op jit(solution)/shard_map/all_to_all | solution.py:142
  12.5 0.7 all-gather.2.cloned.1.call-update
  13.3 1.2 pad_maximum_fusion.2
  14.5 1.1 copy.53
  15.6 1.1 all-to-all-done
  16.7 3.5 %all-to-all-start.1 = ((bf16[4,128,512]{1,0,2:T(4,128)(2,1)}), bf16[4,128,512]{1,0,2:T(4,128)(2,1)S(1)}, u32[]{:S(2)}, u32[]{:S(2)}) async-start(bf16[4,128,512]{1,0,2:T(4,128)(2,1)} %copy.53), calls=%async_computation.1 | async-start | bytes 1048576 | tf_op jit(solution)/shard_map/all_to_all | solution.py:138
  21.5 5.8 %all-to-all-done.1 = bf16[4,128,512]{1,0,2:T(4,128)(2,1)S(1)} async-done(((bf16[4,128,512]{1,0,2:T(4,128)(2,1)}), bf16[4,128,512]{1,0,2:T(4,128)(2,1)S(1)}, u32[]{:S(2)}, u32[]{:S(2)}) %all-to-all-start.1) | async-done | bytes 524320 | tf_op jit(solution)/shard_map/all_to_all | solution.py:138
  28.1 0.7 fusion.4
  32.8 0.6 convolution_bitcast_fusion.1
  33.5 1.2 fusion.45
  34.7 1.2 convolution_subtract_fusion
  35.9 0.6 convolution_add_fusion.2
  36.5 0.6 fusion.13
  37.9 0.6 fusion.20
  39.2 0.6 fusion.23
  39.9 2.8 %collective-permute-start = (f32[2,1,128,128]{3,2,1,0:T(8,128)S(1)}, f32[2,1,128,128]{3,2,1,0:T(8,128)S(1)}, u32[]{:S(2)}, u32[]{:S(2)}) collective-permute-start(f32[2,1,128,128]{3,2,1,0:T(8,128)S(1)} %pad_maximum_fusion.3), channel_id=1, source_target_pairs={{0,4},{4,8},{8,12},{12,16},{16,20},{20,24},{24,28},{28,32},{32,36}... | collective-permute-start | bytes 393224 | tf_op jit(solution)/shard_map/ppermute | solution.py:179
  42.8 0.7 convolution_multiply_fusion.1
  43.5 4.0 %collective-permute-done = f32[2,1,128,128]{3,2,1,0:T(8,128)S(1)} collective-permute-done((f32[2,1,128,128]{3,2,1,0:T(8,128)S(1)}, f32[2,1,128,128]{3,2,1,0:T(8,128)S(1)}, u32[]{:S(2)}, u32[]{:S(2)}) %collective-permute-start) | collective-permute-done | bytes 131104 | tf_op jit(solution)/shard_map/ppermute | solution.py:179
  48.0 2.0 %collective-permute-start.1 = (f32[2,1,128,128]{3,2,1,0:T(8,128)S(1)}, f32[2,1,128,128]{3,2,1,0:T(8,128)S(1)}, u32[]{:S(2)}, u32[]{:S(2)}) collective-permute-start(f32[2,1,128,128]{3,2,1,0:T(8,128)S(1)} %pad_maximum_fusion.4), channel_id=1, source_target_pairs={{0,8},{4,12},{8,16},{12,20},{16,24},{20,28},{24,32},{28,36},{32,40... | collective-permute-start | bytes 393224 | tf_op jit(solution)/shard_map/ppermute | solution.py:179
  50.4 6.7 %collective-permute-done.1 = f32[2,1,128,128]{3,2,1,0:T(8,128)S(1)} collective-permute-done((f32[2,1,128,128]{3,2,1,0:T(8,128)S(1)}, f32[2,1,128,128]{3,2,1,0:T(8,128)S(1)}, u32[]{:S(2)}, u32[]{:S(2)}) %collective-permute-start.1) | collective-permute-done | bytes 131104 | tf_op jit(solution)/shard_map/ppermute | solution.py:179
  57.6 1.3 collective-permute-start.2
  59.0 20.5 %collective-permute-done.2 = f32[2,1,128,128]{3,2,1,0:T(8,128)S(1)} collective-permute-done((f32[2,1,128,128]{3,2,1,0:T(8,128)S(1)}, f32[2,1,128,128]{3,2,1,0:T(8,128)S(1)}, u32[]{:S(2)}, u32[]{:S(2)}) %collective-permute-start.2) | collective-permute-done | bytes 131104 | tf_op jit(solution)/shard_map/ppermute | solution.py:179
  79.6 1.3 collective-permute-start.3
  81.1 12.2 %collective-permute-done.3 = f32[1,128,128]{2,1,0:T(8,128)S(1)} collective-permute-done((f32[1,128,128]{2,1,0:T(8,128)S(1)}, f32[1,128,128]{2,1,0:T(8,128)S(1)}, u32[]{:S(2)}, u32[]{:S(2)}) %collective-permute-start.3) | collective-permute-done | bytes 65568 | tf_op jit(solution)/shard_map/ppermute | solution.py:186
  93.6 1.9 %collective-permute-start.4 = (f32[1,128,128]{2,1,0:T(8,128)S(1)}, f32[1,128,128]{2,1,0:T(8,128)S(1)}, u32[]{:S(2)}, u32[]{:S(2)}) collective-permute-start(f32[1,128,128]{2,1,0:T(8,128)S(1)} %fusion.7), channel_id=1, source_target_pairs={{0,4},{4,8},{8,12},{12,16},{16,20},{20,24},{24,28},{28,32},{32,36}... | collective-permute-start | bytes 196616 | tf_op jit(solution)/shard_map/ppermute | solution.py:190
  95.5 4.3 %collective-permute-done.4 = f32[1,128,128]{2,1,0:T(8,128)S(1)} collective-permute-done((f32[1,128,128]{2,1,0:T(8,128)S(1)}, f32[1,128,128]{2,1,0:T(8,128)S(1)}, u32[]{:S(2)}, u32[]{:S(2)}) %collective-permute-start.4) | collective-permute-done | bytes 65568 | tf_op jit(solution)/shard_map/ppermute | solution.py:190
  101.9 9.3 %all_to_all.34 = bf16[4,512,128]{1,2,0:T(8,128)(2,1)S(1)} all-to-all(bf16[4,512,128]{1,2,0:T(8,128)(2,1)S(1)} %broadcast_in_dim.21), channel_id=1, replica_groups=mesh['heads'=8,'z'=16,'x'=4] {'x'}, dimensions={0} | all-to-all | bytes 1048576 | tf_op jit(solution)/shard_map/all_to_all | solution.py:205
  111.2 2.0 %convolution_convert_fusion = bf16[512,1024]{1,0:T(8,128)(2,1)S(1)} fusion(bf16[512,512]{0,1:T(8,128)(2,1)S(1)} %bitcast.248, bf16[512,1024]{0,1:T(8,128)(2,1)} %all-gather.2.cloned.1.call-done), kind=kOutput, calls=%fused_computation | convolution fusion | flops 537395200 | bytes 2621440 | tf_op jit(solution)/shard_map/dot_general | solution.py:211
  114.3 28.2 %all_to_all.35 = bf16[32,128,2,64]{1,3,2,0:T(8,128)(2,1)S(1)} all-to-all(bf16[32,128,2,64]{1,3,2,0:T(8,128)(2,1)S(1)} %bitcast.233), channel_id=1, replica_groups=mesh['heads'=8,'z'=16,'x'=4] {'x','heads'}, dimensions={0} | all-to-all | bytes 2097152 | tf_op jit(solution)/shard_map/all_to_all | solution.py:217
  142.7 0.8 copy.72
  (83 shorter events, 12.8 us)
Async XLA Ops:
  8.5 8.2 %all-to-all-start = ((f32[3,4,128]{2,0,1:T(4,128)}), f32[3,4,128]{2,0,1:T(4,128)S(1)}, u32[]{:S(2)}, u32[]{:S(2)}) async-start(f32[3,4,128]{2,0,1:T(4,128)} %pad_maximum_fusion.6), calls=%async_computation | async-start | bytes 16384 | tf_op jit(solution)/shard_map/all_to_all | solution.py:142
  12.5 98.7 %all-gather.2.cloned.1.call-start = ((), (), s32[]{:S(2)}) async-start(), calls=%async_computation.4 | async-start | bytes 1114112 | tf_op jit(solution)/shard_map/all_gather | solution.py:210
  16.7 10.6 %all-to-all-start.1 = ((bf16[4,128,512]{1,0,2:T(4,128)(2,1)}), bf16[4,128,512]{1,0,2:T(4,128)(2,1)S(1)}, u32[]{:S(2)}, u32[]{:S(2)}) async-start(bf16[4,128,512]{1,0,2:T(4,128)(2,1)} %copy.53), calls=%async_computation.1 | async-start | bytes 1048576 | tf_op jit(solution)/shard_map/all_to_all | solution.py:138
  39.9 7.6 %collective-permute-start = (f32[2,1,128,128]{3,2,1,0:T(8,128)S(1)}, f32[2,1,128,128]{3,2,1,0:T(8,128)S(1)}, u32[]{:S(2)}, u32[]{:S(2)}) collective-permute-start(f32[2,1,128,128]{3,2,1,0:T(8,128)S(1)} %pad_maximum_fusion.3), channel_id=1, source_target_pairs={{0,4},{4,8},{8,12},{12,16},{16,20},{20,24},{24,28},{28,32},{32,36}... | collective-permute-start | bytes 393224 | tf_op jit(solution)/shard_map/ppermute | solution.py:179
  48.0 9.2 %collective-permute-start.1 = (f32[2,1,128,128]{3,2,1,0:T(8,128)S(1)}, f32[2,1,128,128]{3,2,1,0:T(8,128)S(1)}, u32[]{:S(2)}, u32[]{:S(2)}) collective-permute-start(f32[2,1,128,128]{3,2,1,0:T(8,128)S(1)} %pad_maximum_fusion.4), channel_id=1, source_target_pairs={{0,8},{4,12},{8,16},{12,20},{16,24},{20,28},{24,32},{28,36},{32,40... | collective-permute-start | bytes 393224 | tf_op jit(solution)/shard_map/ppermute | solution.py:179
  57.6 21.8 %collective-permute-start.2 = (f32[2,1,128,128]{3,2,1,0:T(8,128)S(1)}, f32[2,1,128,128]{3,2,1,0:T(8,128)S(1)}, u32[]{:S(2)}, u32[]{:S(2)}) collective-permute-start(f32[2,1,128,128]{3,2,1,0:T(8,128)S(1)} %pad_maximum_fusion.5), channel_id=1, source_target_pairs={{0,16},{4,20},{8,24},{12,28},{16,32},{20,36},{24,40},{28,44},{32,4... | collective-permute-start | bytes 393224 | tf_op jit(solution)/shard_map/ppermute | solution.py:179
  79.6 13.7 %collective-permute-start.3 = (f32[1,128,128]{2,1,0:T(8,128)S(1)}, f32[1,128,128]{2,1,0:T(8,128)S(1)}, u32[]{:S(2)}, u32[]{:S(2)}) collective-permute-start(f32[1,128,128]{2,1,0:T(8,128)S(1)} %bitcast.252), channel_id=1, source_target_pairs={{0,32},{4,36},{8,40},{12,44},{16,48},{20,52},{24,56},{28,60},{1,33... | collective-permute-start | bytes 196616 | tf_op jit(solution)/shard_map/ppermute | solution.py:186
  93.6 6.2 %collective-permute-start.4 = (f32[1,128,128]{2,1,0:T(8,128)S(1)}, f32[1,128,128]{2,1,0:T(8,128)S(1)}, u32[]{:S(2)}, u32[]{:S(2)}) collective-permute-start(f32[1,128,128]{2,1,0:T(8,128)S(1)} %fusion.7), channel_id=1, source_target_pairs={{0,4},{4,8},{8,12},{12,16},{16,20},{20,24},{24,28},{28,32},{32,36}... | collective-permute-start | bytes 196616 | tf_op jit(solution)/shard_map/ppermute | solution.py:190
  100.4 1.2 copy-start
Sparse Core Ops, SparseCore 0:
  15.4 62.5 all-gather.1

commit v5 on v4

--- a/solution.py
+++ b/solution.py
@@ -134,17 +134,33 @@
     key_width = query_proj.shape[1] // head_count
     value_width = value_proj.shape[1] // head_count
 
-    projections = jnp.stack([query_proj, key_proj, value_proj, gate_proj])
-    projections = lax.all_to_all(projections, "x", 2, 1, tiled=True)
-    query_here, key_here, value_here, gate_here = (projections[i] for i in range(4))
+    local_rows = query_proj.shape[0]
+    local_heads = head_count // minor
     resets_wide = jnp.broadcast_to(doc_start.astype(jnp.float32), write_rate.shape)
     per_token = jnp.stack([write_rate, log_decay, resets_wide])
-    per_token = lax.all_to_all(per_token, "x", 1, 2, tiled=True)
+    high = lax.optimization_barrier(per_token.astype(jnp.bfloat16))
+    rest = per_token - high.astype(jnp.float32)
+    middle = lax.optimization_barrier(rest.astype(jnp.bfloat16))
+    low = (rest - middle.astype(jnp.float32)).astype(jnp.bfloat16)
+    exact_parts = jnp.concatenate([high, middle, low])
+    exact_parts = exact_parts.reshape(9, minor, local_heads, local_rows).transpose(3, 1, 0, 2)
+    exact_parts = exact_parts.reshape(local_rows, minor, 9 * local_heads)
+    projections = jnp.stack([query_proj, key_proj, value_proj, gate_proj], axis=1)
+    projections = projections.reshape(local_rows, 4, minor, -1).transpose(0, 2, 1, 3)
+    projections = projections.reshape(local_rows, minor, -1)
+    width = projections.shape[-1]
+    moved = jnp.concatenate([projections, exact_parts], axis=-1)
+    moved = lax.all_to_all(moved, "x", 1, 0, tiled=True)
+    moved = moved.reshape(minor * local_rows, -1)
+    projections = moved[:, :width].reshape(minor * local_rows, 4, -1)
+    query_here, key_here, value_here, gate_here = (projections[:, i] for i in range(4))
+    exact_parts = moved[:, width:].astype(jnp.float32).reshape(minor * local_rows, 3, 3, local_heads)
+    per_token = (exact_parts[:, 0] + exact_parts[:, 1]) + exact_parts[:, 2]
+    per_token = per_token.transpose(1, 2, 0)
     rates_here, decays_here = per_token[0], per_token[1]
     resets_here = per_token[2, 0].astype(jnp.int32)
 
     tok_rows = query_here.shape[0]
-    local_heads = head_count // minor
     blocks = tok_rows // STRETCH
 
     def stretch_major(array, width):

time: 151 us -> 151 us (level)
  the two profiles are of different devices: /device:TPU:385 before, /device:TPU:257 now
where the time goes in v5:
time: 151 us
  waiting for transfers between devices  50.3 us (33%)
  blocking collectives  41.7 us (28%)
  matrix products  17 us (11%)
  between operations  14.1 us (9%)
  starting transfers between devices  14 us (9%)
  local copies, waits for them, and re-layouts  8.5 us (6%)
  other arithmetic  5.31 us (4%)
    all_to_all x1, blocking collectives, on_device(): pieces = lax.all_to_all(pieces, ('x', 'heads'), 0, 0, tiled=True)  28.6 us
    ppermute x3, waiting for transfers between devices, on_device(): got = lax.ppermute(jnp.stack([group_reach, group_saved]), 'z', pairs)  25 us
    all_to_all x1, blocking collectives, on_device(): normed = lax.all_to_all(copies, 'x', 0, 0, tiled=True)  13.1 us
    ppermute x1, waiting for transfers between devices, on_device(): got_saved = lax.ppermute(group_saved, 'z', pairs)  12.4 us
    dot_general x25, matrix products, matrix_product(): jnp.einsum('...de,...ef->...df', left_side, right_side, precision=precise)  9.83 us
    all_to_all x1, waiting for transfers between devices, on_device(): moved = lax.all_to_all(moved, 'x', 1, 0, tiled=True)  7.98 us
    ppermute x3, starting transfers between devices, on_device(): got = lax.ppermute(jnp.stack([group_reach, group_saved]), 'z', pairs)  6.73 us
    unnamed x8, local copies, waits for them, and re-layouts  4.4 us
  transfers between devices with their start and end apart: 7, of which 6 were waited for; matrix products, arithmetic and copies ran while one was open for 13% of the time, Pallas kernels for 0%

profile of v5, /device:TPU:257, one launch (start us, length us, event | category | flops | bytes accessed | tf_op | source)
XLA Modules:
  0.0 151.0 jit_solution(3757905770968537856)
XLA Ops:
  6.5 0.7 convert_element_type.143
  7.2 0.7 fusion.92
  7.9 0.7 fusion.93
  8.6 0.7 subtract_convert_fusion
  9.4 1.0 copy.65
  10.4 1.0 copy.66
  11.4 1.0 copy.67
  12.5 1.0 copy.68
  13.6 0.9 pad_maximum_fusion.2
  14.4 4.0 %all-to-all-start = ((bf16[128,4,521]{0,2,1:T(8,128)(2,1)}), bf16[128,4,521]{0,2,1:T(8,128)(2,1)S(1)}, u32[]{:S(2)}, u32[]{:S(2)}) async-start(bf16[128,4,521]{0,2,1:T(8,128)(2,1)} %pad_maximum_fusion.2), calls=%async_computation | async-start | bytes 1081344 | tf_op jit(solution)/shard_map/all_to_all | solution.py:153
  18.4 0.7 all-gather.2.cloned.1.call-update
  19.3 8.0 %all-to-all-done = bf16[128,4,521]{0,2,1:T(8,128)(2,1)S(1)} async-done(((bf16[128,4,521]{0,2,1:T(8,128)(2,1)}), bf16[128,4,521]{0,2,1:T(8,128)(2,1)S(1)}, u32[]{:S(2)}, u32[]{:S(2)}) %all-to-all-start) | async-done | bytes 533536 | tf_op jit(solution)/shard_map/all_to_all | solution.py:153
  28.9 0.7 fusion.4
  34.9 1.2 fusion.44
  36.3 1.2 convolution_subtract_fusion
  39.5 0.6 fusion.20
  40.9 0.8 fusion.23
  41.7 2.6 %collective-permute-start = (f32[2,1,128,128]{3,2,1,0:T(8,128)S(1)}, f32[2,1,128,128]{3,2,1,0:T(8,128)S(1)}, u32[]{:S(2)}, u32[]{:S(2)}) collective-permute-start(f32[2,1,128,128]{3,2,1,0:T(8,128)S(1)} %pad_maximum_fusion.4), channel_id=1, source_target_pairs={{0,4},{4,8},{8,12},{12,16},{16,20},{20,24},{24,28},{28,32},{32,36}... | collective-permute-start | bytes 393224 | tf_op jit(solution)/shard_map/ppermute | solution.py:195
  44.6 0.7 convolution_multiply_fusion.1
  45.3 3.9 %collective-permute-done = f32[2,1,128,128]{3,2,1,0:T(8,128)S(1)} collective-permute-done((f32[2,1,128,128]{3,2,1,0:T(8,128)S(1)}, f32[2,1,128,128]{3,2,1,0:T(8,128)S(1)}, u32[]{:S(2)}, u32[]{:S(2)}) %collective-permute-start) | collective-permute-done | bytes 131104 | tf_op jit(solution)/shard_map/ppermute | solution.py:195
  49.6 2.2 %collective-permute-start.1 = (f32[2,1,128,128]{3,2,1,0:T(8,128)S(1)}, f32[2,1,128,128]{3,2,1,0:T(8,128)S(1)}, u32[]{:S(2)}, u32[]{:S(2)}) collective-permute-start(f32[2,1,128,128]{3,2,1,0:T(8,128)S(1)} %pad_maximum_fusion.5), channel_id=1, source_target_pairs={{0,8},{4,12},{8,16},{12,20},{16,24},{20,28},{24,32},{28,36},{32,40... | collective-permute-start | bytes 393224 | tf_op jit(solution)/shard_map/ppermute | solution.py:195
  52.2 9.2 %collective-permute-done.1 = f32[2,1,128,128]{3,2,1,0:T(8,128)S(1)} collective-permute-done((f32[2,1,128,128]{3,2,1,0:T(8,128)S(1)}, f32[2,1,128,128]{3,2,1,0:T(8,128)S(1)}, u32[]{:S(2)}, u32[]{:S(2)}) %collective-permute-start.1) | collective-permute-done | bytes 131104 | tf_op jit(solution)/shard_map/ppermute | solution.py:195
  61.8 1.9 %collective-permute-start.2 = (f32[2,1,128,128]{3,2,1,0:T(8,128)S(1)}, f32[2,1,128,128]{3,2,1,0:T(8,128)S(1)}, u32[]{:S(2)}, u32[]{:S(2)}) collective-permute-start(f32[2,1,128,128]{3,2,1,0:T(8,128)S(1)} %pad_maximum_fusion.6), channel_id=1, source_target_pairs={{0,16},{4,20},{8,24},{12,28},{16,32},{20,36},{24,40},{28,44},{32,4... | collective-permute-start | bytes 393224 | tf_op jit(solution)/shard_map/ppermute | solution.py:195
  63.8 12.0 %collective-permute-done.2 = f32[2,1,128,128]{3,2,1,0:T(8,128)S(1)} collective-permute-done((f32[2,1,128,128]{3,2,1,0:T(8,128)S(1)}, f32[2,1,128,128]{3,2,1,0:T(8,128)S(1)}, u32[]{:S(2)}, u32[]{:S(2)}) %collective-permute-start.2) | collective-permute-done | bytes 131104 | tf_op jit(solution)/shard_map/ppermute | solution.py:195
  75.9 1.3 collective-permute-start.3
  77.4 12.4 %collective-permute-done.3 = f32[1,128,128]{2,1,0:T(8,128)S(1)} collective-permute-done((f32[1,128,128]{2,1,0:T(8,128)S(1)}, f32[1,128,128]{2,1,0:T(8,128)S(1)}, u32[]{:S(2)}, u32[]{:S(2)}) %collective-permute-start.3) | collective-permute-done | bytes 65568 | tf_op jit(solution)/shard_map/ppermute | solution.py:202
  90.0 1.9 %collective-permute-start.4 = (f32[1,128,128]{2,1,0:T(8,128)S(1)}, f32[1,128,128]{2,1,0:T(8,128)S(1)}, u32[]{:S(2)}, u32[]{:S(2)}) collective-permute-start(f32[1,128,128]{2,1,0:T(8,128)S(1)} %fusion.7), channel_id=1, source_target_pairs={{0,4},{4,8},{8,12},{12,16},{16,20},{20,24},{24,28},{28,32},{32,36}... | collective-permute-start | bytes 196616 | tf_op jit(solution)/shard_map/ppermute | solution.py:206
  92.0 4.3 %collective-permute-done.4 = f32[1,128,128]{2,1,0:T(8,128)S(1)} collective-permute-done((f32[1,128,128]{2,1,0:T(8,128)S(1)}, f32[1,128,128]{2,1,0:T(8,128)S(1)}, u32[]{:S(2)}, u32[]{:S(2)}) %collective-permute-start.4) | collective-permute-done | bytes 65568 | tf_op jit(solution)/shard_map/ppermute | solution.py:206
  98.4 13.1 %all_to_all.25 = bf16[4,512,128]{1,2,0:T(8,128)(2,1)S(1)} all-to-all(bf16[4,512,128]{1,2,0:T(8,128)(2,1)S(1)} %broadcast_in_dim.24), channel_id=1, replica_groups=mesh['heads'=8,'z'=16,'x'=4] {'x'}, dimensions={0} | all-to-all | bytes 1048576 | tf_op jit(solution)/shard_map/all_to_all | solution.py:221
  111.5 2.0 %convolution_convert_fusion = bf16[512,1024]{1,0:T(8,128)(2,1)S(1)} fusion(bf16[512,512]{0,1:T(8,128)(2,1)S(1)} %bitcast.271, bf16[512,1024]{0,1:T(8,128)(2,1)} %all-gather.2.cloned.1.call-done), kind=kOutput, calls=%fused_computation | convolution fusion | flops 537395200 | bytes 2621440 | tf_op jit(solution)/shard_map/dot_general | solution.py:227
  114.6 28.6 %all_to_all.26 = bf16[32,128,2,64]{1,3,2,0:T(8,128)(2,1)S(1)} all-to-all(bf16[32,128,2,64]{1,3,2,0:T(8,128)(2,1)S(1)} %bitcast.249), channel_id=1, replica_groups=mesh['heads'=8,'z'=16,'x'=4] {'x','heads'}, dimensions={0} | all-to-all | bytes 2097152 | tf_op jit(solution)/shard_map/all_to_all | solution.py:233
  143.3 0.8 copy.91
  (97 shorter events, 15.2 us)
Async XLA Ops:
  14.4 12.8 %all-to-all-start = ((bf16[128,4,521]{0,2,1:T(8,128)(2,1)}), bf16[128,4,521]{0,2,1:T(8,128)(2,1)S(1)}, u32[]{:S(2)}, u32[]{:S(2)}) async-start(bf16[128,4,521]{0,2,1:T(8,128)(2,1)} %pad_maximum_fusion.2), calls=%async_computation | async-start | bytes 1081344 | tf_op jit(solution)/shard_map/all_to_all | solution.py:153
  18.4 93.0 %all-gather.2.cloned.1.call-start = ((), (), s32[]{:S(2)}) async-start(), calls=%async_computation.3 | async-start | bytes 1114112 | tf_op jit(solution)/shard_map/all_gather | solution.py:226
  41.7 7.4 %collective-permute-start = (f32[2,1,128,128]{3,2,1,0:T(8,128)S(1)}, f32[2,1,128,128]{3,2,1,0:T(8,128)S(1)}, u32[]{:S(2)}, u32[]{:S(2)}) collective-permute-start(f32[2,1,128,128]{3,2,1,0:T(8,128)S(1)} %pad_maximum_fusion.4), channel_id=1, source_target_pairs={{0,4},{4,8},{8,12},{12,16},{16,20},{20,24},{24,28},{28,32},{32,36}... | collective-permute-start | bytes 393224 | tf_op jit(solution)/shard_map/ppermute | solution.py:195
  49.6 11.8 %collective-permute-start.1 = (f32[2,1,128,128]{3,2,1,0:T(8,128)S(1)}, f32[2,1,128,128]{3,2,1,0:T(8,128)S(1)}, u32[]{:S(2)}, u32[]{:S(2)}) collective-permute-start(f32[2,1,128,128]{3,2,1,0:T(8,128)S(1)} %pad_maximum_fusion.5), channel_id=1, source_target_pairs={{0,8},{4,12},{8,16},{12,20},{16,24},{20,28},{24,32},{28,36},{32,40... | collective-permute-start | bytes 393224 | tf_op jit(solution)/shard_map/ppermute | solution.py:195
  61.8 13.9 %collective-permute-start.2 = (f32[2,1,128,128]{3,2,1,0:T(8,128)S(1)}, f32[2,1,128,128]{3,2,1,0:T(8,128)S(1)}, u32[]{:S(2)}, u32[]{:S(2)}) collective-permute-start(f32[2,1,128,128]{3,2,1,0:T(8,128)S(1)} %pad_maximum_fusion.6), channel_id=1, source_target_pairs={{0,16},{4,20},{8,24},{12,28},{16,32},{20,36},{24,40},{28,44},{32,4... | collective-permute-start | bytes 393224 | tf_op jit(solution)/shard_map/ppermute | solution.py:195
  75.9 13.9 %collective-permute-start.3 = (f32[1,128,128]{2,1,0:T(8,128)S(1)}, f32[1,128,128]{2,1,0:T(8,128)S(1)}, u32[]{:S(2)}, u32[]{:S(2)}) collective-permute-start(f32[1,128,128]{2,1,0:T(8,128)S(1)} %bitcast.279), channel_id=1, source_target_pairs={{0,32},{4,36},{8,40},{12,44},{16,48},{20,52},{24,56},{28,60},{1,33... | collective-permute-start | bytes 196616 | tf_op jit(solution)/shard_map/ppermute | solution.py:202
  90.0 6.2 %collective-permute-start.4 = (f32[1,128,128]{2,1,0:T(8,128)S(1)}, f32[1,128,128]{2,1,0:T(8,128)S(1)}, u32[]{:S(2)}, u32[]{:S(2)}) collective-permute-start(f32[1,128,128]{2,1,0:T(8,128)S(1)} %fusion.7), channel_id=1, source_target_pairs={{0,4},{4,8},{8,12},{12,16},{16,20},{20,24},{24,28},{28,32},{32,36}... | collective-permute-start | bytes 196616 | tf_op jit(solution)/shard_map/ppermute | solution.py:206
  97.5 0.7 copy-start
Sparse Core Ops, SparseCore 0:
  21.3 64.1 all-gather.1

commit v6 on v4

--- a/solution.py
+++ b/solution.py
@@ -11,7 +11,7 @@
 JOINT_A2A = True
 
 
-precise = lax.Precision.HIGHEST
+precise = lax.Precision.HIGH
 epsilon = 1e-06
 
 

time: 151 us -> 145 us (0.960)
  waiting for transfers between devices: 55.3 us -> 49.1 us
  blocking collectives: 37.5 us -> 42.9 us
  matrix products: 16.9 us -> 11.9 us
    ppermute x3, waiting for transfers between devices: 31.2 us -> 24.5 us  [on_device(): got = lax.ppermute(jnp.stack([group_reach, group_saved]), 'z', pairs)]
    all_to_all x1, blocking collectives: 9.33 us -> 13.2 us  [on_device(): normed = lax.all_to_all(copies, 'x', 0, 0, tiled=True)]
    dot_general x25, matrix products: 9.66 us -> 6.44 us  [matrix_product(): jnp.einsum('...de,...ef->...df', left_side, right_side, precision=precise)]
  transfers between devices with their start and end apart: 8 -> 8, of which waited for: 7 -> 7; matrix products, arithmetic and copies ran while one was open for 14% -> 11% of each run, Pallas kernels for 0% -> 0%
where the time goes in v6:
time: 145 us; the launch traced here: 144 us
  waiting for transfers between devices  49.1 us (34%)
  blocking collectives  42.9 us (30%)
  starting transfers between devices  16.6 us (11%)
  between operations  14 us (10%)
  matrix products  11.9 us (8%)
  local copies, waits for them, and re-layouts  4.95 us (3%)
  other arithmetic  4.83 us (3%)
    all_to_all x1, blocking collectives, on_device(): pieces = lax.all_to_all(pieces, ('x', 'heads'), 0, 0, tiled=True)  29.7 us
    ppermute x3, waiting for transfers between devices, on_device(): got = lax.ppermute(jnp.stack([group_reach, group_saved]), 'z', pairs)  24.5 us
    all_to_all x1, blocking collectives, on_device(): normed = lax.all_to_all(copies, 'x', 0, 0, tiled=True)  13.2 us
    ppermute x1, waiting for transfers between devices, on_device(): got_saved = lax.ppermute(group_saved, 'z', pairs)  12.5 us
    dot_general x25, matrix products, matrix_product(): jnp.einsum('...de,...ef->...df', left_side, right_side, precision=precise)  6.44 us
    ppermute x3, starting transfers between devices, on_device(): got = lax.ppermute(jnp.stack([group_reach, group_saved]), 'z', pairs)  5.86 us
    all_to_all x1, waiting for transfers between devices, on_device(): projections = lax.all_to_all(projections, 'x', 2, 1, tiled=True)  5.79 us
    ppermute x1, waiting for transfers between devices, on_device(): lax.ppermute(group_saved, 'z', [(i, i + 1) for i in range(major - 1)])  4.55 us
  transfers between devices with their start and end apart: 8, of which 7 were waited for; matrix products, arithmetic and copies ran while one was open for 11% of the time, Pallas kernels for 0%

profile of v6, /device:TPU:385, one launch (start us, length us, event | category | flops | bytes accessed | tf_op | source)
XLA Modules:
  0.0 144.2 jit_solution(7436729373558068567)
XLA Ops:
  6.5 0.7 convert_element_type.142
  7.2 1.3 pad_maximum_fusion.6
  8.5 4.0 %all-to-all-start = ((f32[3,4,128]{2,0,1:T(4,128)}), f32[3,4,128]{2,0,1:T(4,128)S(1)}, u32[]{:S(2)}, u32[]{:S(2)}) async-start(f32[3,4,128]{2,0,1:T(4,128)} %pad_maximum_fusion.6), calls=%async_computation | async-start | bytes 16384 | tf_op jit(solution)/shard_map/all_to_all | solution.py:142
  12.5 0.7 all-gather.2.cloned.1.call-update
  13.3 1.2 pad_maximum_fusion.2
  14.5 1.1 copy.53
  15.6 1.1 all-to-all-done
  16.7 3.5 %all-to-all-start.1 = ((bf16[4,128,512]{1,0,2:T(4,128)(2,1)}), bf16[4,128,512]{1,0,2:T(4,128)(2,1)S(1)}, u32[]{:S(2)}, u32[]{:S(2)}) async-start(bf16[4,128,512]{1,0,2:T(4,128)(2,1)} %copy.53), calls=%async_computation.1 | async-start | bytes 1048576 | tf_op jit(solution)/shard_map/all_to_all | solution.py:138
  21.5 5.8 %all-to-all-done.1 = bf16[4,128,512]{1,0,2:T(4,128)(2,1)S(1)} async-done(((bf16[4,128,512]{1,0,2:T(4,128)(2,1)}), bf16[4,128,512]{1,0,2:T(4,128)(2,1)S(1)}, u32[]{:S(2)}, u32[]{:S(2)}) %all-to-all-start.1) | async-done | bytes 524320 | tf_op jit(solution)/shard_map/all_to_all | solution.py:138
  27.3 0.4 copy.54
  28.1 0.5 fusion.4
  31.6 0.4 convolution_bitcast_fusion.1
  32.0 0.8 fusion.45
  32.8 0.8 convolution_subtract_fusion
  34.8 0.4 fusion.20
  36.0 2.7 %collective-permute-start = (f32[2,1,128,128]{3,2,1,0:T(8,128)S(1)}, f32[2,1,128,128]{3,2,1,0:T(8,128)S(1)}, u32[]{:S(2)}, u32[]{:S(2)}) collective-permute-start(f32[2,1,128,128]{3,2,1,0:T(8,128)S(1)} %pad_maximum_fusion.3), channel_id=1, source_target_pairs={{0,4},{4,8},{8,12},{12,16},{16,20},{20,24},{24,28},{28,32},{32,36}... | collective-permute-start | bytes 393224 | tf_op jit(solution)/shard_map/ppermute | solution.py:179
  38.8 0.5 convolution_multiply_fusion.1
  39.2 4.0 %collective-permute-done = f32[2,1,128,128]{3,2,1,0:T(8,128)S(1)} collective-permute-done((f32[2,1,128,128]{3,2,1,0:T(8,128)S(1)}, f32[2,1,128,128]{3,2,1,0:T(8,128)S(1)}, u32[]{:S(2)}, u32[]{:S(2)}) %collective-permute-start) | collective-permute-done | bytes 131104 | tf_op jit(solution)/shard_map/ppermute | solution.py:179
  43.6 1.9 %collective-permute-start.1 = (f32[2,1,128,128]{3,2,1,0:T(8,128)S(1)}, f32[2,1,128,128]{3,2,1,0:T(8,128)S(1)}, u32[]{:S(2)}, u32[]{:S(2)}) collective-permute-start(f32[2,1,128,128]{3,2,1,0:T(8,128)S(1)} %pad_maximum_fusion.4), channel_id=1, source_target_pairs={{0,8},{4,12},{8,16},{12,20},{16,24},{20,28},{24,32},{28,36},{32,40... | collective-permute-start | bytes 393224 | tf_op jit(solution)/shard_map/ppermute | solution.py:179
  45.9 6.6 %collective-permute-done.1 = f32[2,1,128,128]{3,2,1,0:T(8,128)S(1)} collective-permute-done((f32[2,1,128,128]{3,2,1,0:T(8,128)S(1)}, f32[2,1,128,128]{3,2,1,0:T(8,128)S(1)}, u32[]{:S(2)}, u32[]{:S(2)}) %collective-permute-start.1) | collective-permute-done | bytes 131104 | tf_op jit(solution)/shard_map/ppermute | solution.py:179
  52.8 1.3 collective-permute-start.2
  54.2 13.8 %collective-permute-done.2 = f32[2,1,128,128]{3,2,1,0:T(8,128)S(1)} collective-permute-done((f32[2,1,128,128]{3,2,1,0:T(8,128)S(1)}, f32[2,1,128,128]{3,2,1,0:T(8,128)S(1)}, u32[]{:S(2)}, u32[]{:S(2)}) %collective-permute-start.2) | collective-permute-done | bytes 131104 | tf_op jit(solution)/shard_map/ppermute | solution.py:179
  68.2 1.3 collective-permute-start.3
  69.7 12.5 %collective-permute-done.3 = f32[1,128,128]{2,1,0:T(8,128)S(1)} collective-permute-done((f32[1,128,128]{2,1,0:T(8,128)S(1)}, f32[1,128,128]{2,1,0:T(8,128)S(1)}, u32[]{:S(2)}, u32[]{:S(2)}) %collective-permute-start.3) | collective-permute-done | bytes 65568 | tf_op jit(solution)/shard_map/ppermute | solution.py:186
  82.4 1.9 %collective-permute-start.4 = (f32[1,128,128]{2,1,0:T(8,128)S(1)}, f32[1,128,128]{2,1,0:T(8,128)S(1)}, u32[]{:S(2)}, u32[]{:S(2)}) collective-permute-start(f32[1,128,128]{2,1,0:T(8,128)S(1)} %fusion.7), channel_id=1, source_target_pairs={{0,4},{4,8},{8,12},{12,16},{16,20},{20,24},{24,28},{28,32},{32,36}... | collective-permute-start | bytes 196616 | tf_op jit(solution)/shard_map/ppermute | solution.py:190
  84.3 4.5 %collective-permute-done.4 = f32[1,128,128]{2,1,0:T(8,128)S(1)} collective-permute-done((f32[1,128,128]{2,1,0:T(8,128)S(1)}, f32[1,128,128]{2,1,0:T(8,128)S(1)}, u32[]{:S(2)}, u32[]{:S(2)}) %collective-permute-start.4) | collective-permute-done | bytes 65568 | tf_op jit(solution)/shard_map/ppermute | solution.py:190
  88.9 0.4 fusion.1
  90.4 13.2 %all_to_all.34 = bf16[4,512,128]{1,2,0:T(8,128)(2,1)S(1)} all-to-all(bf16[4,512,128]{1,2,0:T(8,128)(2,1)S(1)} %broadcast_in_dim.21), channel_id=1, replica_groups=mesh['heads'=8,'z'=16,'x'=4] {'x'}, dimensions={0} | all-to-all | bytes 1048576 | tf_op jit(solution)/shard_map/all_to_all | solution.py:205
  103.6 2.0 %convolution_convert_fusion = bf16[512,1024]{1,0:T(8,128)(2,1)S(1)} fusion(bf16[512,512]{0,1:T(8,128)(2,1)S(1)} %bitcast.248, bf16[512,1024]{0,1:T(8,128)(2,1)} %all-gather.2.cloned.1.call-done), kind=kOutput, calls=%fused_computation | convolution fusion | flops 537395200 | bytes 2621440 | tf_op jit(solution)/shard_map/dot_general | solution.py:211
  105.6 0.5 copy.69
  106.7 29.7 %all_to_all.35 = bf16[32,128,2,64]{1,3,2,0:T(8,128)(2,1)S(1)} all-to-all(bf16[32,128,2,64]{1,3,2,0:T(8,128)(2,1)S(1)} %bitcast.233), channel_id=1, replica_groups=mesh['heads'=8,'z'=16,'x'=4] {'x','heads'}, dimensions={0} | all-to-all | bytes 2097152 | tf_op jit(solution)/shard_map/all_to_all | solution.py:217
  136.6 0.8 copy.72
  (83 shorter events, 10.1 us)
Async XLA Ops:
  8.5 8.2 %all-to-all-start = ((f32[3,4,128]{2,0,1:T(4,128)}), f32[3,4,128]{2,0,1:T(4,128)S(1)}, u32[]{:S(2)}, u32[]{:S(2)}) async-start(f32[3,4,128]{2,0,1:T(4,128)} %pad_maximum_fusion.6), calls=%async_computation | async-start | bytes 16384 | tf_op jit(solution)/shard_map/all_to_all | solution.py:142
  12.5 91.1 %all-gather.2.cloned.1.call-start = ((), (), s32[]{:S(2)}) async-start(), calls=%async_computation.4 | async-start | bytes 1114112 | tf_op jit(solution)/shard_map/all_gather | solution.py:210
  16.7 10.6 %all-to-all-start.1 = ((bf16[4,128,512]{1,0,2:T(4,128)(2,1)}), bf16[4,128,512]{1,0,2:T(4,128)(2,1)S(1)}, u32[]{:S(2)}, u32[]{:S(2)}) async-start(bf16[4,128,512]{1,0,2:T(4,128)(2,1)} %copy.53), calls=%async_computation.1 | async-start | bytes 1048576 | tf_op jit(solution)/shard_map/all_to_all | solution.py:138
  36.0 7.2 %collective-permute-start = (f32[2,1,128,128]{3,2,1,0:T(8,128)S(1)}, f32[2,1,128,128]{3,2,1,0:T(8,128)S(1)}, u32[]{:S(2)}, u32[]{:S(2)}) collective-permute-start(f32[2,1,128,128]{3,2,1,0:T(8,128)S(1)} %pad_maximum_fusion.3), channel_id=1, source_target_pairs={{0,4},{4,8},{8,12},{12,16},{16,20},{20,24},{24,28},{28,32},{32,36}... | collective-permute-start | bytes 393224 | tf_op jit(solution)/shard_map/ppermute | solution.py:179
  43.6 8.8 %collective-permute-start.1 = (f32[2,1,128,128]{3,2,1,0:T(8,128)S(1)}, f32[2,1,128,128]{3,2,1,0:T(8,128)S(1)}, u32[]{:S(2)}, u32[]{:S(2)}) collective-permute-start(f32[2,1,128,128]{3,2,1,0:T(8,128)S(1)} %pad_maximum_fusion.4), channel_id=1, source_target_pairs={{0,8},{4,12},{8,16},{12,20},{16,24},{20,28},{24,32},{28,36},{32,40... | collective-permute-start | bytes 393224 | tf_op jit(solution)/shard_map/ppermute | solution.py:179
  52.8 15.2 %collective-permute-start.2 = (f32[2,1,128,128]{3,2,1,0:T(8,128)S(1)}, f32[2,1,128,128]{3,2,1,0:T(8,128)S(1)}, u32[]{:S(2)}, u32[]{:S(2)}) collective-permute-start(f32[2,1,128,128]{3,2,1,0:T(8,128)S(1)} %pad_maximum_fusion.5), channel_id=1, source_target_pairs={{0,16},{4,20},{8,24},{12,28},{16,32},{20,36},{24,40},{28,44},{32,4... | collective-permute-start | bytes 393224 | tf_op jit(solution)/shard_map/ppermute | solution.py:179
  68.2 14.0 %collective-permute-start.3 = (f32[1,128,128]{2,1,0:T(8,128)S(1)}, f32[1,128,128]{2,1,0:T(8,128)S(1)}, u32[]{:S(2)}, u32[]{:S(2)}) collective-permute-start(f32[1,128,128]{2,1,0:T(8,128)S(1)} %bitcast.252), channel_id=1, source_target_pairs={{0,32},{4,36},{8,40},{12,44},{16,48},{20,52},{24,56},{28,60},{1,33... | collective-permute-start | bytes 196616 | tf_op jit(solution)/shard_map/ppermute | solution.py:186
  82.4 6.5 %collective-permute-start.4 = (f32[1,128,128]{2,1,0:T(8,128)S(1)}, f32[1,128,128]{2,1,0:T(8,128)S(1)}, u32[]{:S(2)}, u32[]{:S(2)}) collective-permute-start(f32[1,128,128]{2,1,0:T(8,128)S(1)} %fusion.7), channel_id=1, source_target_pairs={{0,4},{4,8},{8,12},{12,16},{16,20},{20,24},{24,28},{28,32},{32,36}... | collective-permute-start | bytes 196616 | tf_op jit(solution)/shard_map/ppermute | solution.py:190
  89.3 0.8 copy-start
Sparse Core Ops, SparseCore 0:
  15.4 63.5 all-gather.1
